TPU v7x, 128 devices: a whole 4x4x4 slice. The times are simulated.
128 devices in a mesh: row: 8 (over x_lo, z), col: 16 (over y, x_hi, core).
Axes of the slice: x: 4 (x_hi: 2, x_lo: 2; x = x_hi * 2 + x_lo), y: 4, z: 4, core: 2. Of those that a mesh axis runs over, the one named last changes fastest.
Arguments:
- amplitudes: bfloat16 [768, 640000], P('col', 'row'), may hold values from -6 to 6
- integrals: bfloat16 [640000, 1600], P(('row', 'col')), may hold values from -0.0078125 to 0.0078125
- occ_irrep: int32 [120], replicated, may hold values from 0 to 7, as said below
- vir_irrep: int32 [800], replicated, may hold values from 0 to 7, as said below
- tile_owner: int32 [384], replicated, may hold values from 0 to 127, as said below
Outputs:
- inbox: bfloat16 [1536, 1600], P(('row', 'col'))
Inputs may be any that keep to these rules, and one draw needn't show every extreme that they name: `tile_owner`: no device owns more than 6 tiles and some device owns exactly 6; in every draw the 3 tiles of some device's rows of result all have one owner. `occ_irrep`: labels never decrease along the orbitals, so each irrep's orbitals form one contiguous block. Each of irreps 1 to 7 holds at least one and at most 2 orbitals, one of them exactly that most; irrep 0 holds all the others. `vir_irrep`: labels never decrease along the orbitals, so each irrep's orbitals form one contiguous block. Each of irreps 1 to 7 holds at least one and at most 13 orbitals, one of them exactly that most; irrep 0 holds all the others.
All inputs are finite; a program needn't handle non-finite values.
Results may differ from a plain program's by a relative error of at most 0.0014.
Values may be sent and summed in bfloat16 or wider, within the bound.
No kernel may reach another device: no remote copies, remote signals or barrier semaphores. Data moves between devices by JAX's collectives and lax.ppermute only.
A program may use at most 192 MiB of HBM per device.

v0:
```python
import jax
import jax.numpy as jnp
from jax import lax
from jax.sharding import PartitionSpec as P

TR = 2
TILES_DEV = 3
CAP = 6


def lookup(table, index):
    entries = table.shape[0]
    hits = index[:, None] == jnp.arange(entries, dtype=jnp.int32)[None, :]
    return jnp.sum(jnp.where(hits, table[None, :], 0), axis=1)


def on_device(amplitudes, integrals, occ_irrep, vir_irrep, tile_owner):
    ncols = lax.axis_size("col")
    nrows = lax.axis_size("row")
    devices = nrows * ncols
    myself = lax.axis_index("row") * ncols + lax.axis_index("col")
    cd_dev = integrals.shape[0]
    ab_width = integrals.shape[1]
    local_pairs = amplitudes.shape[0]
    pair_count = local_pairs * ncols
    norb = occ_irrep.shape[0]
    nvirt = vir_irrep.shape[0]
    pair_index = jnp.arange(pair_count, dtype=jnp.int32)
    pair_irrep = jnp.bitwise_xor(
        lookup(occ_irrep, pair_index // norb), lookup(occ_irrep, pair_index % norb)
    )
    ab_index = jnp.arange(ab_width, dtype=jnp.int32)
    ab_irrep = jnp.bitwise_xor(
        lookup(vir_irrep, ab_index // nvirt), lookup(vir_irrep, ab_index % nvirt)
    )
    zero_half = jnp.zeros((), jnp.bfloat16)
    panel = lax.all_to_all(amplitudes, "col", split_axis=1, concat_axis=0, tiled=True)
    width = panel.shape[1]
    cd_index = myself * cd_dev + jnp.arange(width, dtype=jnp.int32)
    cd_irrep = jnp.bitwise_xor(
        lookup(vir_irrep, cd_index // nvirt), lookup(vir_irrep, cd_index % nvirt)
    )
    masked_t = jnp.where(pair_irrep[:, None] == cd_irrep[None, :], panel, zero_half)
    masked_v = jnp.where(cd_irrep[:, None] == ab_irrep[None, :], integrals, zero_half)
    ntiles = tile_owner.shape[0]
    tile_ids = jnp.arange(ntiles, dtype=jnp.int32)
    same = tile_owner[:, None] == tile_owner[None, :]
    earlier = tile_ids[:, None] > tile_ids[None, :]
    rank = jnp.sum(jnp.where(same & earlier, 1, 0), axis=1).astype(jnp.int32)
    slot = tile_owner * CAP + rank
    masked_t, masked_v = (masked_t, masked_v)
    total = jnp.dot(masked_t, masked_v, preferred_element_type=jnp.float32)
    summed = lax.psum_scatter(total, ("row", "col"), scatter_dimension=0, tiled=True).astype(
        jnp.bfloat16
    )
    my_tiles = summed.reshape(TILES_DEV, TR * ab_width)
    my_ids = myself * TILES_DEV + jnp.arange(TILES_DEV, dtype=jnp.int32)
    my_owner = lookup(tile_owner, my_ids)
    target = my_owner[None, :] == jnp.arange(devices, dtype=jnp.int32)[:, None]
    outgoing = jnp.where(target[:, :, None], my_tiles[None, :, :], zero_half)
    arrived = lax.all_to_all(outgoing, ("row", "col"), split_axis=0, concat_axis=0, tiled=True)
    picker = (slot[None, :] == myself * CAP + jnp.arange(CAP, dtype=jnp.int32)[:, None]).astype(
        jnp.bfloat16
    )
    placed = jnp.dot(
        picker, arrived.reshape(ntiles, TR * ab_width), preferred_element_type=jnp.float32
    )
    return placed.astype(jnp.bfloat16).reshape(CAP * TR, ab_width)


def solution(mesh):
    in_specs = (P("col", "row"), P(("row", "col"), None), P(), P(), P())
    out_specs = P(("row", "col"), None)
    return jax.shard_map(
        on_device, mesh=mesh, in_specs=in_specs, out_specs=out_specs, check_vma=False
    )
```

profile of v0, /device:TPU:0, one launch (start us, length us, event | category | flops | bytes accessed | tf_op | source)
XLA Modules:
  0.0 311.9 jit_solution(1720189224727886846)
XLA Ops:
  0.0 14.5 %all_to_all.17 = bf16[48,16,5000]{2,1,0:T(8,128)(2,1)} reshape(bf16[48,80000]{1,0:T(8,128)(2,1)} %param.5) | data formatting | bytes 15360000 | tf_op jit(solution)/shard_map/all_to_all | solution.py:37
  14.5 10.7 %copy.8 = bf16[48,16,5000]{2,0,1:T(8,128)(2,1)} copy(bf16[48,16,5000]{2,1,0:T(8,128)(2,1)} %all_to_all.17) | data formatting | bytes 15360000 | tf_op jit(solution)/shard_map/all_to_all | solution.py:37
  25.2 0.0 copy-start.1
  25.2 0.0 copy-start.2
  25.2 0.0 copy-start
  25.2 7.3 %all-to-all-start = ((bf16[48,16,5000]{2,0,1:T(8,128)(2,1)}), bf16[48,16,5000]{2,0,1:T(8,128)(2,1)}, u32[]{:S(2)}, u32[]{:S(2)}) async-start(bf16[48,16,5000]{2,0,1:T(8,128)(2,1)} %copy.8), calls=%async_computation | async-start | bytes 15728640 | tf_op jit(solution)/shard_map/all_to_all | solution.py:37
  32.6 0.0 copy-done.1
  32.6 4.9 %select_reduce_fusion = (s32[5000]{0:T(1024)S(1)}, s32[5000]{0:T(1024)S(1)}) fusion(s32[5000]{0:T(1024)S(1)} %get-tuple-element.11, s32[800]{0:T(1024)S(1)} %copy-done.1, s32[5000]{0:T(1024)S(1)} %get-tuple-element.12), kind=kLoop, calls=%fused_computation.3 | loop fusion | flops 23990000 | bytes 83200 | tf_op jit(solution)/shard_map/reduce_sum | solution.py:14
  37.5 1.9 select_reduce_fusion.2
  39.4 0.0 copy-done.2
  39.5 0.2 select_reduce_fusion.5
  39.7 0.0 copy-done
  39.7 0.2 select_reduce_fusion.7
  39.9 83.7 %all-to-all-done = bf16[48,16,5000]{2,0,1:T(8,128)(2,1)} async-done(((bf16[48,16,5000]{2,0,1:T(8,128)(2,1)}), bf16[48,16,5000]{2,0,1:T(8,128)(2,1)}, u32[]{:S(2)}, u32[]{:S(2)}) %all-to-all-start) | async-done | bytes 7680032 | tf_op jit(solution)/shard_map/all_to_all | solution.py:37
  123.6 24.3 %fusion = f32[768,1600]{1,0:T(8,128)} fusion(bf16[5000,1600]{0,1:T(8,128)(2,1)} %param.6, s32[5000]{0:T(1024)S(1)} %xor.26, s32[1600]{0:T(1024)S(1)} %xor.27, bf16[768,5000]{1,0:T(8,128)(2,1)} %bitcast.1, s32[768]{0:T(1024)S(1)} %xor.25), kind=kOutput, calls=%fused_computation.1 | convolution fusion | flops 12311680000 | bytes 28624672 | tf_op jit(solution)/shard_map/dot_general | solution.py:52
  148.0 107.4 %all-reduce.2 = bf16[768,1600]{1,0:T(8,128)(2,1)S(1)} all-reduce(f32[768,1600]{1,0:T(8,128)} %fusion), channel_id=2, replica_groups=mesh['row'=8,'col'=16] {'row','col'}, use_global_device_ids=true, to_apply=%region_8.9.clone | all-reduce | flops 1228800 | bytes 7372800
  255.4 0.1 broadcast_in_dim.145
  255.5 2.9 broadcast_select_fusion
  258.4 4.7 %all-to-all-start.1 = ((bf16[128,3,3200]{2,1,0:T(4,128)(2,1)}), bf16[128,3,3200]{2,1,0:T(4,128)(2,1)S(1)}, u32[]{:S(2)}, u32[]{:S(2)}) async-start(bf16[128,3,3200]{2,1,0:T(4,128)(2,1)} %broadcast_select_fusion), calls=%async_computation.1 | async-start | bytes 6553600 | tf_op jit(solution)/shard_map/all_to_all | solution.py:61
  263.1 0.2 select_reduce_fusion.4
  263.4 41.4 %all-to-all-done.1 = bf16[128,3,3200]{2,1,0:T(4,128)(2,1)S(1)} async-done(((bf16[128,3,3200]{2,1,0:T(4,128)(2,1)}), bf16[128,3,3200]{2,1,0:T(4,128)(2,1)S(1)}, u32[]{:S(2)}, u32[]{:S(2)}) %all-to-all-start.1) | async-done | bytes 2457632 | tf_op jit(solution)/shard_map/all_to_all | solution.py:61
  304.8 4.2 %reshape.118 = bf16[384,3200]{1,0:T(8,128)(2,1)} reshape(bf16[128,3,3200]{2,1,0:T(4,128)(2,1)S(1)} %all-to-all-done.1) | data formatting | bytes 4915200 | tf_op jit(solution)/shard_map/reshape | solution.py:66
  309.0 2.2 convolution_convert_fusion
  311.2 0.7 reshape.119
  (11 shorter events, 0.1 us)
Async XLA Ops:
  25.2 7.4 %copy-start.1 = (s32[800]{0:T(1024)S(1)}, s32[800]{0:T(1024)}, u32[]{:S(2)}) copy-start(s32[800]{0:T(1024)} %param.8) | copy-start | bytes 9604
  25.2 14.3 %copy-start.2 = (s32[120]{0:T(128)S(1)}, s32[120]{0:T(128)}, u32[]{:S(2)}) copy-start(s32[120]{0:T(128)} %param.7) | copy-start | bytes 1444
  25.2 14.5 %copy-start = (s32[384]{0:T(512)S(1)}, s32[384]{0:T(512)}, u32[]{:S(2)}) copy-start(s32[384]{0:T(512)} %param.9) | copy-start | bytes 4612
  25.2 98.5 %all-to-all-start = ((bf16[48,16,5000]{2,0,1:T(8,128)(2,1)}), bf16[48,16,5000]{2,0,1:T(8,128)(2,1)}, u32[]{:S(2)}, u32[]{:S(2)}) async-start(bf16[48,16,5000]{2,0,1:T(8,128)(2,1)} %copy.8), calls=%async_computation | async-start | bytes 15728640 | tf_op jit(solution)/shard_map/all_to_all | solution.py:37
  258.4 46.3 %all-to-all-start.1 = ((bf16[128,3,3200]{2,1,0:T(4,128)(2,1)}), bf16[128,3,3200]{2,1,0:T(4,128)(2,1)S(1)}, u32[]{:S(2)}, u32[]{:S(2)}) async-start(bf16[128,3,3200]{2,1,0:T(4,128)(2,1)} %broadcast_select_fusion), calls=%async_computation.1 | async-start | bytes 6553600 | tf_op jit(solution)/shard_map/all_to_all | solution.py:61
where the time goes:
time: 313 us; the launch traced here: 312 us
  waiting for transfers between devices  125 us (40%)
  blocking collectives  107 us (34%)
  local copies, waits for them, and re-layouts  30.3 us (10%)
  matrix products  26.5 us (8%)
  starting transfers between devices  12 us (4%)
  other arithmetic  10.4 us (3%)
    unnamed x1, blocking collectives  107 us
    all_to_all x1, waiting for transfers between devices, on_device(): lax.all_to_all(amplitudes, 'col', split_axis=1, concat_axis=0, tiled=True)  83.7 us
    all_to_all x1, waiting for transfers between devices, on_device(): lax.all_to_all(outgoing, ('row', 'col'), split_axis=0, concat_axis=0, til...  41.4 us
    all_to_all x2, local copies, waits for them, and re-layouts, on_device(): lax.all_to_all(amplitudes, 'col', split_axis=1, concat_axis=0, tiled=True)  25.2 us
    dot_general x1, matrix products, on_device(): total = jnp.dot(masked_t, masked_v, preferred_element_type=jnp.float32)  24.3 us
    all_to_all x1, starting transfers between devices, on_device(): lax.all_to_all(amplitudes, 'col', split_axis=1, concat_axis=0, tiled=True)  7.33 us
    reduce_sum x4, other arithmetic, lookup(): return jnp.sum(jnp.where(hits, table[None, :], 0), axis=1)  7.17 us
  transfers between devices with their start and end apart: 2, of which 2 were waited for; matrix products, arithmetic and copies ran while one was open for 2% of the time, Pallas kernels for 0%

commit v1 on v0

--- a/solution.py
+++ b/solution.py
@@ -48,24 +48,19 @@
     earlier = tile_ids[:, None] > tile_ids[None, :]
     rank = jnp.sum(jnp.where(same & earlier, 1, 0), axis=1).astype(jnp.int32)
     slot = tile_owner * CAP + rank
-    masked_t, masked_v = (masked_t, masked_v)
     total = jnp.dot(masked_t, masked_v, preferred_element_type=jnp.float32)
-    summed = lax.psum_scatter(total, ("row", "col"), scatter_dimension=0, tiled=True).astype(
-        jnp.bfloat16
-    )
-    my_tiles = summed.reshape(TILES_DEV, TR * ab_width)
-    my_ids = myself * TILES_DEV + jnp.arange(TILES_DEV, dtype=jnp.int32)
-    my_owner = lookup(tile_owner, my_ids)
-    target = my_owner[None, :] == jnp.arange(devices, dtype=jnp.int32)[:, None]
-    outgoing = jnp.where(target[:, :, None], my_tiles[None, :, :], zero_half)
-    arrived = lax.all_to_all(outgoing, ("row", "col"), split_axis=0, concat_axis=0, tiled=True)
-    picker = (slot[None, :] == myself * CAP + jnp.arange(CAP, dtype=jnp.int32)[:, None]).astype(
-        jnp.bfloat16
-    )
-    placed = jnp.dot(
-        picker, arrived.reshape(ntiles, TR * ab_width), preferred_element_type=jnp.float32
-    )
-    return placed.astype(jnp.bfloat16).reshape(CAP * TR, ab_width)
+    chunk = total.size // devices
+    flat = total.reshape(devices, chunk // 128, 128)
+    summed = lax.psum_scatter(flat, ("row", "col"), scatter_dimension=0, tiled=True)
+    my_tiles = summed.astype(jnp.bfloat16).reshape(TILES_DEV, TR * ab_width)
+    every = lax.all_gather(my_tiles, ("row", "col"), axis=0, tiled=True)
+    wanted = myself * CAP + jnp.arange(CAP, dtype=jnp.int32)
+    match = slot[None, :] == wanted[:, None]
+    source = jnp.sum(jnp.where(match, tile_ids[None, :], 0), axis=1)
+    found = jnp.any(match, axis=1)
+    picked = jnp.take(every, source, axis=0)
+    placed = jnp.where(found[:, None], picked, zero_half)
+    return placed.reshape(CAP * TR, ab_width)
 
 
 def solution(mesh):

time: 313 us -> 1020 us (3.26)
  waiting for transfers between devices: 125 us -> 926 us
  blocking collectives: 107 us -> 0 us
  between operations: 0.17 us -> 13.6 us
    reduce_scatter x0 -> x1, waiting for transfers between devices: none -> 652 us  [on_device(): lax.psum_scatter(flat, ('row', 'col'), scatter_dimension=0, tiled=True)]
    all_gather x0 -> x1, waiting for transfers between devices: none -> 190 us  [on_device(): every = lax.all_gather(my_tiles, ('row', 'col'), axis=0, tiled=True)]
    unnamed x1 -> x0, blocking collectives: 107 us -> none
    all_to_all x1 -> x0, waiting for transfers between devices: 41.4 us -> none  [on_device(): lax.all_to_all(outgoing, ('row', 'col'), split_axis=0, concat_axis=0, til...]
  transfers between devices with their start and end apart: 2 -> 3, of which waited for: 2 -> 3; matrix products, arithmetic and copies ran while one was open for 2% -> 1% of each run, Pallas kernels for 0% -> 0%
where the time goes in v1:
time: 1020 us
  waiting for transfers between devices  926 us (91%)
  local copies, waits for them, and re-layouts  39.4 us (4%)
  matrix products  24.2 us (2%)
  between operations  13.6 us (1%)
    reduce_scatter x1, waiting for transfers between devices, on_device(): lax.psum_scatter(flat, ('row', 'col'), scatter_dimension=0, tiled=True)  652 us
    all_gather x1, waiting for transfers between devices, on_device(): every = lax.all_gather(my_tiles, ('row', 'col'), axis=0, tiled=True)  190 us
    all_to_all x1, waiting for transfers between devices, on_device(): lax.all_to_all(amplitudes, 'col', split_axis=1, concat_axis=0, tiled=True)  83.8 us
    all_to_all x2, local copies, waits for them, and re-layouts, on_device(): lax.all_to_all(amplitudes, 'col', split_axis=1, concat_axis=0, tiled=True)  25.2 us
    dot_general x1, matrix products, on_device(): total = jnp.dot(masked_t, masked_v, preferred_element_type=jnp.float32)  24.2 us
  transfers between devices with their start and end apart: 3, of which 3 were waited for; matrix products, arithmetic and copies ran while one was open for 1% of the time, Pallas kernels for 0%

profile of v1, /device:TPU:0, one launch (start us, length us, event | category | flops | bytes accessed | tf_op | source)
XLA Modules:
  0.0 1019.8 jit_solution(6275446370411667435)
XLA Ops:
  6.5 14.5 %all_to_all.14 = bf16[48,16,5000]{2,1,0:T(8,128)(2,1)} reshape(bf16[48,80000]{1,0:T(8,128)(2,1)} %param.5) | data formatting | bytes 15360000 | tf_op jit(solution)/shard_map/all_to_all | solution.py:37
  21.0 10.7 %copy.10 = bf16[48,16,5000]{2,0,1:T(8,128)(2,1)} copy(bf16[48,16,5000]{2,1,0:T(8,128)(2,1)} %all_to_all.14) | data formatting | bytes 15360000 | tf_op jit(solution)/shard_map/all_to_all | solution.py:37
  31.7 0.0 copy-start.1
  31.7 0.0 copy-start.2
  31.7 7.3 all-to-all-start
  39.0 0.2 reduce-scatter.2.cloned.1.call-start
  39.3 0.0 copy-done.1
  39.3 4.9 select_reduce_fusion
  44.2 1.9 select_reduce_fusion.2
  46.2 0.0 copy-done.2
  46.2 0.2 select_reduce_fusion.5
  46.4 83.8 %all-to-all-done = bf16[48,16,5000]{2,0,1:T(8,128)(2,1)} async-done(((bf16[48,16,5000]{2,0,1:T(8,128)(2,1)}), bf16[48,16,5000]{2,0,1:T(8,128)(2,1)}, u32[]{:S(2)}, u32[]{:S(2)}) %all-to-all-start) | async-done | bytes 7680032 | tf_op jit(solution)/shard_map/all_to_all | solution.py:37
  130.2 24.2 %fusion = f32[768,1600]{1,0:T(8,128)} fusion(bf16[5000,1600]{0,1:T(8,128)(2,1)} %param.6, s32[5000]{0:T(1024)S(1)} %xor.26, s32[1600]{0:T(1024)S(1)} %xor.27, bf16[768,5000]{1,0:T(8,128)(2,1)} %bitcast.1, s32[768]{0:T(1024)S(1)} %xor.25), kind=kOutput, calls=%fused_computation.2 | convolution fusion | flops 12311680000 | bytes 28624672 | tf_op jit(solution)/shard_map/dot_general | solution.py:51
  154.3 0.0 copy-start
  154.3 7.2 reshape.117
  161.5 0.0 reduce-scatter.2.cloned.1.call-update
  161.5 0.0 all-gather.3.cloned.1.call-start
  161.6 652.0 %reduce-scatter.2.cloned.1.call-done = f32[1,75,128]{2,1,0:T(8,128)} async-done(((f32[128,75,128]{2,1,0:T(8,128)}), f32[1,75,128]{2,1,0:T(8,128)}) %reduce-scatter.2.cloned.1.call-update) | async-done | bytes 38416 | tf_op jit(solution)/shard_map/reduce_scatter | solution.py:54
  813.6 0.8 convert_element_type.3
  814.4 0.6 reshape.127
  815.0 0.0 all-gather.3.cloned.1.call-update
  815.1 0.0 copy-done
  815.1 0.2 select_reduce_fusion.4
  815.3 0.2 fusion.17
  815.5 0.1 broadcast_in_dim.143
  815.6 0.1 broadcast_in_dim.144
  815.7 0.2 compare_reduce_fusion
  815.9 0.1 broadcast_in_dim.138
  815.9 0.1 broadcast_in_dim.139
  816.0 190.1 %all-gather.3.cloned.1.call-done = bf16[128,3,3200]{2,1,0:T(4,128)(2,1)} async-done(((bf16[1,3,3200]{2,1,0:T(4,128)(2,1)}), bf16[128,3,3200]{2,1,0:T(4,128)(2,1)}) %all-gather.3.cloned.1.call-update) | async-done | bytes 2457616 | tf_op jit(solution)/shard_map/all_gather | solution.py:56
  1006.1 5.4 reshape.128
  1011.5 0.6 gather_fusion
  1012.1 0.1 gather.7
  1012.2 0.7 select_select_fusion
  (11 shorter events, 0.1 us)
Async XLA Ops:
  31.7 7.6 copy-start.1
  31.7 14.5 %copy-start.2 = (s32[120]{0:T(128)S(1)}, s32[120]{0:T(128)}, u32[]{:S(2)}) copy-start(s32[120]{0:T(128)} %param.7) | copy-start | bytes 1444
  31.7 98.5 %all-to-all-start = ((bf16[48,16,5000]{2,0,1:T(8,128)(2,1)}), bf16[48,16,5000]{2,0,1:T(8,128)(2,1)}, u32[]{:S(2)}, u32[]{:S(2)}) async-start(bf16[48,16,5000]{2,0,1:T(8,128)(2,1)} %copy.10), calls=%async_computation | async-start | bytes 15728640 | tf_op jit(solution)/shard_map/all_to_all | solution.py:37
  39.0 774.6 %reduce-scatter.2.cloned.1.call-start = ((), (), s32[]{:S(2)}) async-start(), calls=%async_computation.2 | async-start | bytes 5283840 | tf_op jit(solution)/shard_map/reduce_scatter | solution.py:54
  154.3 660.7 %copy-start = (s32[384]{0:T(512)S(1)}, s32[384]{0:T(512)}, u32[]{:S(2)}) copy-start(s32[384]{0:T(512)} %param.9) | copy-start | bytes 4612
  161.5 844.6 %all-gather.3.cloned.1.call-start = ((), (), s32[]{:S(2)}) async-start(), calls=%async_computation.3 | async-start | bytes 3302400 | tf_op jit(solution)/shard_map/all_gather | solution.py:56
Sparse Core Ops, SparseCore 0:
  161.7 651.9 reduce-scatter.1
  815.3 190.7 all-gather.2

commit v2 on v1

--- a/solution.py
+++ b/solution.py
@@ -49,16 +49,13 @@
     rank = jnp.sum(jnp.where(same & earlier, 1, 0), axis=1).astype(jnp.int32)
     slot = tile_owner * CAP + rank
     total = jnp.dot(masked_t, masked_v, preferred_element_type=jnp.float32)
-    chunk = total.size // devices
-    flat = total.reshape(devices, chunk // 128, 128)
-    summed = lax.psum_scatter(flat, ("row", "col"), scatter_dimension=0, tiled=True)
-    my_tiles = summed.astype(jnp.bfloat16).reshape(TILES_DEV, TR * ab_width)
-    every = lax.all_gather(my_tiles, ("row", "col"), axis=0, tiled=True)
+    summed = lax.psum(total, ("row", "col"))
+    every = summed.reshape(ntiles, TR * ab_width)
     wanted = myself * CAP + jnp.arange(CAP, dtype=jnp.int32)
     match = slot[None, :] == wanted[:, None]
     source = jnp.sum(jnp.where(match, tile_ids[None, :], 0), axis=1)
     found = jnp.any(match, axis=1)
-    picked = jnp.take(every, source, axis=0)
+    picked = jnp.take(every, source, axis=0).astype(jnp.bfloat16)
     placed = jnp.where(found[:, None], picked, zero_half)
     return placed.reshape(CAP * TR, ab_width)
 

time: 1020 us -> 264 us (0.26)
  waiting for transfers between devices: 926 us -> 83 us
  blocking collectives: 0 us -> 108 us
  between operations: 13.6 us -> 0.15 us
    reduce_scatter x1 -> x0, waiting for transfers between devices: 652 us -> none  [on_device(): lax.psum_scatter(flat, ('row', 'col'), scatter_dimension=0, tiled=True)]
    all_gather x1 -> x0, waiting for transfers between devices: 190 us -> none  [on_device(): every = lax.all_gather(my_tiles, ('row', 'col'), axis=0, tiled=True)]
    psum x0 -> x1, blocking collectives: none -> 108 us  [on_device(): summed = lax.psum(total, ('row', 'col'))]
  transfers between devices with their start and end apart: 3 -> 1, of which waited for: 3 -> 1; matrix products, arithmetic and copies ran while one was open for 1% -> 3% of each run, Pallas kernels for 0% -> 0%
where the time goes in v2:
time: 264 us; the launch traced here: 263 us
  blocking collectives  108 us (41%)
  waiting for transfers between devices  83 us (31%)
  local copies, waits for them, and re-layouts  32.4 us (12%)
  matrix products  24.2 us (9%)
  other arithmetic  8.4 us (3%)
  starting transfers between devices  7.33 us (3%)
    psum x1, blocking collectives, on_device(): summed = lax.psum(total, ('row', 'col'))  108 us
    all_to_all x1, waiting for transfers between devices, on_device(): lax.all_to_all(amplitudes, 'col', split_axis=1, concat_axis=0, tiled=True)  83 us
    all_to_all x2, local copies, waits for them, and re-layouts, on_device(): lax.all_to_all(amplitudes, 'col', split_axis=1, concat_axis=0, tiled=True)  25.2 us
    dot_general x1, matrix products, on_device(): total = jnp.dot(masked_t, masked_v, preferred_element_type=jnp.float32)  24.2 us
    all_to_all x1, starting transfers between devices, on_device(): lax.all_to_all(amplitudes, 'col', split_axis=1, concat_axis=0, tiled=True)  7.33 us
    reduce_sum x3, other arithmetic, lookup(): return jnp.sum(jnp.where(hits, table[None, :], 0), axis=1)  6.99 us
    reshape x1, local copies, waits for them, and re-layouts, on_device(): every = summed.reshape(ntiles, TR * ab_width)  6.16 us
  transfers between devices with their start and end apart: 1, of which 1 were waited for; matrix products, arithmetic and copies ran while one was open for 3% of the time, Pallas kernels for 0%

profile of v2, /device:TPU:0, one launch (start us, length us, event | category | flops | bytes accessed | tf_op | source)
XLA Modules:
  0.0 263.1 jit_solution(14452806865200523135)
XLA Ops:
  0.0 14.5 %all_to_all.14 = bf16[48,16,5000]{2,1,0:T(8,128)(2,1)} reshape(bf16[48,80000]{1,0:T(8,128)(2,1)} %param.5) | data formatting | bytes 15360000 | tf_op jit(solution)/shard_map/all_to_all | solution.py:37
  14.5 10.7 %copy.8 = bf16[48,16,5000]{2,0,1:T(8,128)(2,1)} copy(bf16[48,16,5000]{2,1,0:T(8,128)(2,1)} %all_to_all.14) | data formatting | bytes 15360000 | tf_op jit(solution)/shard_map/all_to_all | solution.py:37
  25.2 0.0 copy-start
  25.2 0.0 copy-start.1
  25.2 0.0 copy-start.2
  25.2 7.3 %all-to-all-start = ((bf16[48,16,5000]{2,0,1:T(8,128)(2,1)}), bf16[48,16,5000]{2,0,1:T(8,128)(2,1)}, u32[]{:S(2)}, u32[]{:S(2)}) async-start(bf16[48,16,5000]{2,0,1:T(8,128)(2,1)} %copy.8), calls=%async_computation | async-start | bytes 15728640 | tf_op jit(solution)/shard_map/all_to_all | solution.py:37
  32.5 0.0 copy-done
  32.5 0.2 select_reduce_fusion.4
  32.8 0.2 fusion.18
  33.0 0.1 broadcast_in_dim.143
  33.1 0.1 broadcast_in_dim.144
  33.1 0.2 compare_reduce_fusion
  33.3 0.1 broadcast_in_dim.138
  33.4 0.1 broadcast_in_dim.139
  33.5 0.0 copy-done.1
  33.5 4.9 %select_reduce_fusion = (s32[5000]{0:T(1024)S(1)}, s32[5000]{0:T(1024)S(1)}) fusion(s32[5000]{0:T(1024)S(1)} %get-tuple-element.11, s32[800]{0:T(1024)S(1)} %copy-done.1, s32[5000]{0:T(1024)S(1)} %get-tuple-element.12), kind=kLoop, calls=%fused_computation.4 | loop fusion | flops 23990000 | bytes 83200 | tf_op jit(solution)/shard_map/reduce_sum | solution.py:14
  38.5 1.9 select_reduce_fusion.2
  40.4 0.0 copy-done.2
  40.4 0.2 select_reduce_fusion.5
  40.7 83.0 %all-to-all-done = bf16[48,16,5000]{2,0,1:T(8,128)(2,1)} async-done(((bf16[48,16,5000]{2,0,1:T(8,128)(2,1)}), bf16[48,16,5000]{2,0,1:T(8,128)(2,1)}, u32[]{:S(2)}, u32[]{:S(2)}) %all-to-all-start) | async-done | bytes 7680032 | tf_op jit(solution)/shard_map/all_to_all | solution.py:37
  123.6 24.2 %fusion = f32[768,1600]{1,0:T(8,128)} fusion(bf16[5000,1600]{0,1:T(8,128)(2,1)} %param.6, s32[5000]{0:T(1024)S(1)} %xor.26, s32[1600]{0:T(1024)S(1)} %xor.27, bf16[768,5000]{1,0:T(8,128)(2,1)} %bitcast.1, s32[768]{0:T(1024)S(1)} %xor.25), kind=kOutput, calls=%fused_computation.2 | convolution fusion | flops 12311680000 | bytes 28624672 | tf_op jit(solution)/shard_map/dot_general | solution.py:51
  147.8 6.2 %reshape.114 = f32[384,3200]{1,0:T(8,128)} reshape(f32[768,1600]{1,0:T(8,128)} %fusion) | data formatting | bytes 9830400 | tf_op jit(solution)/shard_map/reshape | solution.py:53
  154.0 107.8 %all-reduce.1 = bf16[384,3200]{1,0:T(8,128)(2,1)S(1)} all-reduce(f32[384,3200]{1,0:T(8,128)} %reshape.114), channel_id=1, replica_groups=mesh['row'=8,'col'=16] {'row','col'}, use_global_device_ids=true, to_apply=%region_9.10 | all-reduce | flops 1228800 | bytes 7372800 | tf_op jit(solution)/shard_map/psum | solution.py:52
  261.7 0.6 gather_fusion
  262.3 0.1 gather.7
  262.4 0.7 fusion.8
  (11 shorter events, 0.1 us)
Async XLA Ops:
  25.2 7.4 %copy-start = (s32[384]{0:T(512)S(1)}, s32[384]{0:T(512)}, u32[]{:S(2)}) copy-start(s32[384]{0:T(512)} %param.9) | copy-start | bytes 4612
  25.2 8.4 %copy-start.1 = (s32[800]{0:T(1024)S(1)}, s32[800]{0:T(1024)}, u32[]{:S(2)}) copy-start(s32[800]{0:T(1024)} %param.8) | copy-start | bytes 9604
  25.2 15.3 %copy-start.2 = (s32[120]{0:T(128)S(1)}, s32[120]{0:T(128)}, u32[]{:S(2)}) copy-start(s32[120]{0:T(128)} %param.7) | copy-start | bytes 1444
  25.2 98.5 %all-to-all-start = ((bf16[48,16,5000]{2,0,1:T(8,128)(2,1)}), bf16[48,16,5000]{2,0,1:T(8,128)(2,1)}, u32[]{:S(2)}, u32[]{:S(2)}) async-start(bf16[48,16,5000]{2,0,1:T(8,128)(2,1)} %copy.8), calls=%async_computation | async-start | bytes 15728640 | tf_op jit(solution)/shard_map/all_to_all | solution.py:37

commit v3 on v2

v3 whole, which is shorter than its diff:
```python
import jax
import jax.numpy as jnp
from jax import lax
from jax.sharding import PartitionSpec as P

TR = 2
TILES_DEV = 3
CAP = 6
PIECES = 2


def lookup(table, index):
    return jnp.take(table, index, axis=0, mode="clip")


def on_device(amplitudes, integrals, occ_irrep, vir_irrep, tile_owner):
    ncols = lax.axis_size("col")
    nrows = lax.axis_size("row")
    myself = lax.axis_index("row") * ncols + lax.axis_index("col")
    cd_dev = integrals.shape[0]
    ab_width = integrals.shape[1]
    local_pairs = amplitudes.shape[0]
    pair_count = local_pairs * ncols
    norb = occ_irrep.shape[0]
    nvirt = vir_irrep.shape[0]
    pair_index = jnp.arange(pair_count, dtype=jnp.int32)
    pair_irrep = jnp.bitwise_xor(
        lookup(occ_irrep, pair_index // norb), lookup(occ_irrep, pair_index % norb)
    )
    ab_index = jnp.arange(ab_width, dtype=jnp.int32)
    ab_irrep = jnp.bitwise_xor(
        lookup(vir_irrep, ab_index // nvirt), lookup(vir_irrep, ab_index % nvirt)
    )
    zero_half = jnp.zeros((), jnp.bfloat16)
    piece = cd_dev // PIECES
    split = amplitudes.reshape(local_pairs, ncols, PIECES, piece)
    total = None
    for h in range(PIECES):
        part = split[:, :, h, :].reshape(local_pairs, ncols * piece)
        panel = lax.all_to_all(part, "col", split_axis=1, concat_axis=0, tiled=True)
        cd_index = myself * cd_dev + h * piece + jnp.arange(piece, dtype=jnp.int32)
        cd_irrep = jnp.bitwise_xor(
            lookup(vir_irrep, cd_index // nvirt), lookup(vir_irrep, cd_index % nvirt)
        )
        slab = integrals[h * piece:(h + 1) * piece]
        masked_t = jnp.where(pair_irrep[:, None] == cd_irrep[None, :], panel, zero_half)
        masked_v = jnp.where(cd_irrep[:, None] == ab_irrep[None, :], slab, zero_half)
        term = jnp.dot(masked_t, masked_v, preferred_element_type=jnp.float32)
        total = term if total is None else total + term
    ntiles = tile_owner.shape[0]
    tile_ids = jnp.arange(ntiles, dtype=jnp.int32)
    same = tile_owner[:, None] == tile_owner[None, :]
    earlier = tile_ids[:, None] > tile_ids[None, :]
    rank = jnp.sum(jnp.where(same & earlier, 1, 0), axis=1).astype(jnp.int32)
    slot = tile_owner * CAP + rank
    summed = lax.psum(total, ("row", "col"))
    wanted = myself * CAP + jnp.arange(CAP, dtype=jnp.int32)
    match = slot[None, :] == wanted[:, None]
    source = jnp.sum(jnp.where(match, tile_ids[None, :], 0), axis=1)
    found = jnp.any(match, axis=1)
    rows = (source[:, None] * TR + jnp.arange(TR, dtype=jnp.int32)[None, :]).reshape(CAP * TR)
    keep = jnp.repeat(found, TR)
    picked = jnp.take(summed, rows, axis=0).astype(jnp.bfloat16)
    placed = jnp.where(keep[:, None], picked, zero_half)
    return placed.reshape(CAP * TR, ab_width)


def solution(mesh):
    in_specs = (P("col", "row"), P(("row", "col"), None), P(), P(), P())
    out_specs = P(("row", "col"), None)
    return jax.shard_map(
        on_device, mesh=mesh, in_specs=in_specs, out_specs=out_specs, check_vma=False
    )
```

time: 264 us -> 306 us (1.16)
  local copies, waits for them, and re-layouts: 32.4 us -> 115 us
  waiting for transfers between devices: 83 us -> 39.2 us
  other arithmetic: 8.4 us -> 2.15 us
  starting transfers between devices: 7.33 us -> 11.7 us
  matrix products: 24.2 us -> 28.1 us
    gather x2 -> x9, local copies, waits for them, and re-layouts: 0.7 us -> 62.1 us  [the longest x8 59.4 us: lookup(): return jnp.take(table, index, axis=0, mode='clip')]
    all_to_all x1 -> x2, waiting for transfers between devices: 83 us -> 39.2 us  [on_device(): panel = lax.all_to_all(part, 'col', split_axis=1, concat_axis=0, tiled=True)]
    slice x0 -> x1, local copies, waits for them, and re-layouts: none -> 20.4 us  [on_device(): part = split[:, :, h, :].reshape(local_pairs, ncols * piece)]
    all_to_all x2, local copies, waits for them, and re-layouts: 25.2 us -> 15.4 us  [on_device(): panel = lax.all_to_all(part, 'col', split_axis=1, concat_axis=0, tiled=True)]
    reduce_sum x3 -> x0, other arithmetic: 6.99 us -> none  [lookup(): return jnp.sum(jnp.where(hits, table[None, :], 0), axis=1)]
    reshape x1, local copies, waits for them, and re-layouts: 6.16 us -> 12.7 us  [on_device(): split = amplitudes.reshape(local_pairs, ncols, PIECES, piece)]
    all_to_all x1 -> x2, starting transfers between devices: 7.33 us -> 11.7 us  [on_device(): panel = lax.all_to_all(part, 'col', split_axis=1, concat_axis=0, tiled=True)]
    psum x0 -> x1, local copies, waits for them, and re-layouts: none -> 3.98 us  [on_device(): summed = lax.psum(total, ('row', 'col'))]
  transfers between devices with their start and end apart: 1 -> 2, of which waited for: 1 -> 1; matrix products, arithmetic and copies ran while one was open for 3% -> 27% of each run, Pallas kernels for 0% -> 0%
where the time goes in v3:
time: 306 us
  local copies, waits for them, and re-layouts  115 us (38%)
  blocking collectives  110 us (36%)
  waiting for transfers between devices  39.2 us (13%)
  matrix products  28.1 us (9%)
  starting transfers between devices  11.7 us (4%)
    psum x1, blocking collectives, on_device(): summed = lax.psum(total, ('row', 'col'))  110 us
    gather x8, local copies, waits for them, and re-layouts, lookup(): return jnp.take(table, index, axis=0, mode='clip')  59.4 us
    all_to_all x2, waiting for transfers between devices, on_device(): panel = lax.all_to_all(part, 'col', split_axis=1, concat_axis=0, tiled=True)  39.2 us
    dot_general x2, matrix products, on_device(): term = jnp.dot(masked_t, masked_v, preferred_element_type=jnp.float32)  28.1 us
    slice x1, local copies, waits for them, and re-layouts, on_device(): part = split[:, :, h, :].reshape(local_pairs, ncols * piece)  20.4 us
    all_to_all x2, local copies, waits for them, and re-layouts, on_device(): panel = lax.all_to_all(part, 'col', split_axis=1, concat_axis=0, tiled=True)  15.4 us
    reshape x1, local copies, waits for them, and re-layouts, on_device(): split = amplitudes.reshape(local_pairs, ncols, PIECES, piece)  12.7 us
    all_to_all x2, starting transfers between devices, on_device(): panel = lax.all_to_all(part, 'col', split_axis=1, concat_axis=0, tiled=True)  11.7 us
  transfers between devices with their start and end apart: 2, of which 1 were waited for; matrix products, arithmetic and copies ran while one was open for 27% of the time, Pallas kernels for 0%

profile of v3, /device:TPU:0, one launch (start us, length us, event | category | flops | bytes accessed | tf_op | source)
XLA Modules:
  0.0 305.9 jit_solution(248784186909955609)
XLA Ops:
  0.0 0.0 copy-start
  0.0 12.7 %reshape.274 = bf16[48,16,2,2500]{3,2,1,0:T(2,128)(2,1)} reshape(bf16[48,80000]{1,0:T(8,128)(2,1)} %param.5) | data formatting | bytes 15360000 | tf_op jit(solution)/shard_map/reshape | solution.py:36
  12.7 20.4 %fusion.33 = (bf16[48,16,1,2500]{3,2,1,0:T(2,128)(2,1)}, bf16[48,16,1,2500]{3,2,1,0:T(2,128)(2,1)S(1)}) fusion(bf16[48,16,2,2500]{3,2,1,0:T(2,128)(2,1)} %reshape.274), kind=kLoop, calls=%fused_computation.85 | loop fusion | bytes 15360000 | tf_op jit(solution)/shard_map/slice | solution.py:39
  33.0 6.1 %copy.24 = bf16[48,16,1,2500]{3,0,1,2:T(8,128)(2,1)} copy(bf16[48,16,1,2500]{3,2,1,0:T(2,128)(2,1)S(1)} %get-tuple-element.6) | data formatting | bytes 7680000 | tf_op jit(solution)/shard_map/all_to_all | solution.py:40
  39.2 7.2 %all-to-all-start = ((bf16[48,16,2500]{2,0,1:T(8,128)(2,1)}), bf16[48,16,2500]{2,0,1:T(8,128)(2,1)}, u32[]{:S(2)}, u32[]{:S(2)}) async-start(bf16[48,16,2500]{2,0,1:T(8,128)(2,1)} %bitcast.15), calls=%async_computation | async-start | bytes 7864320 | tf_op jit(solution)/shard_map/all_to_all | solution.py:40
  46.4 0.0 copy-start.3
  46.4 9.3 %copy.23 = bf16[48,16,1,2500]{3,0,1,2:T(8,128)(2,1)} copy(bf16[48,16,1,2500]{3,2,1,0:T(2,128)(2,1)} %get-tuple-element.5) | data formatting | bytes 7680000 | tf_op jit(solution)/shard_map/all_to_all | solution.py:40
  55.7 0.0 copy-done.3
  55.7 0.2 select_reduce_fusion
  56.0 0.2 fusion.19
  56.2 39.2 %all-to-all-done = bf16[48,16,2500]{2,0,1:T(8,128)(2,1)} async-done(((bf16[48,16,2500]{2,0,1:T(8,128)(2,1)}), bf16[48,16,2500]{2,0,1:T(8,128)(2,1)}, u32[]{:S(2)}, u32[]{:S(2)}) %all-to-all-start) | async-done | bytes 3840032 | tf_op jit(solution)/shard_map/all_to_all | solution.py:40
  95.4 4.5 %all-to-all-start.1 = ((bf16[48,16,2500]{2,0,1:T(8,128)(2,1)}), bf16[48,16,2500]{2,0,1:T(8,128)(2,1)}, u32[]{:S(2)}, u32[]{:S(2)}) async-start(bf16[48,16,2500]{2,0,1:T(8,128)(2,1)} %bitcast.14), calls=%async_computation.1 | async-start | bytes 7864320 | tf_op jit(solution)/shard_map/all_to_all | solution.py:40
  99.9 0.1 iota_add_fusion.2
  100.0 0.1 add.203
  100.1 0.1 add.191
  100.1 0.1 fusion.20
  100.3 0.0 copy-done
  100.3 9.4 %gather_fusion.2 = s32[2500]{0:T(1024)S(1)} fusion(s32[800]{0:T(1024)S(1)} %copy-done, s32[3072]{0:T(1024)S(1)} %pad_clamp_fusion.3), kind=kCustom, calls=%fused_computation.2 | custom fusion | bytes 30000 | tf_op jit(solution)/shard_map/jit(_take)/gather | solution.py:13
  109.7 9.4 %gather_fusion.3 = s32[2500]{0:T(1024)S(1)} fusion(s32[800]{0:T(1024)S(1)} %copy-done, s32[3072]{0:T(1024)S(1)} %pad_clamp_fusion.2), kind=kCustom, calls=%fused_computation.3 | custom fusion | bytes 30000 | tf_op jit(solution)/shard_map/jit(_take)/gather | solution.py:13
  119.1 0.1 fusion.27
  119.2 0.0 copy-start.2
  119.2 6.1 %gather_fusion.4 = s32[1600]{0:T(1024)S(1)} fusion(s32[800]{0:T(1024)S(1)} %copy-done, s32[2048]{0:T(1024)S(1)} %pad_clamp_fusion.5), kind=kCustom, calls=%fused_computation.4 | custom fusion | bytes 19200 | tf_op jit(solution)/shard_map/jit(_take)/gather | solution.py:13
  125.3 0.3 fusion.26
  125.6 6.1 %gather_fusion.5 = s32[1600]{0:T(1024)S(1)} fusion(s32[800]{0:T(1024)S(1)} %copy-done, s32[2048]{0:T(1024)S(1)} %pad_clamp_fusion.4), kind=kCustom, calls=%fused_computation.5 | custom fusion | bytes 19200 | tf_op jit(solution)/shard_map/jit(_take)/gather | solution.py:13
  131.8 0.0 copy-done.2
  131.8 4.8 %gather_fusion = s32[768]{0:T(1024)S(1)} fusion(s32[120]{0:T(128)S(1)} %copy-done.2, s32[1024]{0:T(1024)S(1)} %pad_clamp_fusion.8), kind=kCustom, calls=%fused_computation | custom fusion | bytes 9216 | tf_op jit(solution)/shard_map/jit(_take)/gather | solution.py:13
  136.7 4.8 %gather_fusion.1 = s32[768]{0:T(1024)S(1)} fusion(s32[120]{0:T(128)S(1)} %copy-done.2, s32[1024]{0:T(1024)S(1)} %pad_clamp_fusion.7), kind=kCustom, calls=%fused_computation.1 | custom fusion | bytes 9216 | tf_op jit(solution)/shard_map/jit(_take)/gather | solution.py:13
  141.5 0.1 fusion.21
  141.6 9.4 %gather_fusion.6 = s32[2500]{0:T(1024)S(1)} fusion(s32[800]{0:T(1024)S(1)} %copy-done, s32[3072]{0:T(1024)S(1)} %pad_clamp_fusion.1), kind=kCustom, calls=%fused_computation.6 | custom fusion | bytes 30000 | tf_op jit(solution)/shard_map/jit(_take)/gather | solution.py:13
  151.0 9.4 %gather_fusion.7 = s32[2500]{0:T(1024)S(1)} fusion(s32[800]{0:T(1024)S(1)} %copy-done, s32[3072]{0:T(1024)S(1)} %pad_clamp_fusion), kind=kCustom, calls=%fused_computation.7 | custom fusion | bytes 30000 | tf_op jit(solution)/shard_map/jit(_take)/gather | solution.py:13
  160.4 0.2 compare_reduce_fusion
  160.6 0.1 broadcast_in_dim.87
  160.7 0.1 broadcast_in_dim.88
  160.9 12.5 %fusion = f32[768,1600]{0,1:T(8,128)} fusion(bf16[5000,1600]{0,1:T(8,128)(2,1)} %param.6, s32[2500]{0:T(1024)S(1)} %xor.37, s32[1600]{0:T(1024)S(1)} %xor.38, bf16[768,2500]{1,0:T(8,128)(2,1)} %bitcast.2, s32[768]{0:T(1024)S(1)} %xor.36), kind=kOutput, calls=%fused_computation.11 | convolution fusion | flops 6155840000 | bytes 17076224 | tf_op jit(solution)/shard_map/dot_general | solution.py:48
  173.4 0.0 all-to-all-done.1
  173.4 0.0 copy-start.1
  173.4 15.6 %fusion.10 = f32[768,1600]{0,1:T(8,128)} fusion(f32[768,1600]{0,1:T(8,128)} %fusion, bf16[5000,1600]{0,1:T(8,128)(2,1)} %param.6, s32[2500]{0:T(1024)S(1)} %xor.39, s32[1600]{0:T(1024)S(1)} %xor.38, bf16[768,2500]{1,0:T(8,128)(2,1)} %bitcast.5, s32[768]{0:T(1024)S(1)} %xor.36), kind=kOutput, calls=%fused_computation.23 | convolution fusion | flops 6157068800 | bytes 21991424 | tf_op jit(solution)/shard_map/dot_general | solution.py:48
  189.0 109.5 %all-reduce.1 = bf16[768,1600]{0,1:T(8,128)(2,1)S(1)} all-reduce(f32[768,1600]{0,1:T(8,128)} %fusion.10), channel_id=1, replica_groups=mesh['row'=8,'col'=16] {'row','col'}, use_global_device_ids=true, to_apply=%region_3.4 | all-reduce | flops 1228800 | bytes 7372800 | tf_op jit(solution)/shard_map/psum | solution.py:56
  298.5 4.0 %copy.18 = bf16[768,1600]{1,0:T(8,128)(2,1)} copy(bf16[768,1600]{0,1:T(8,128)(2,1)S(1)} %all-reduce.1) | data formatting | bytes 4915200 | tf_op jit(solution)/shard_map/psum | solution.py:56
  302.5 2.7 gather_fusion.8
  305.2 0.7 fusion.18
  305.9 0.0 copy-done.1
  (20 shorter events, 0.2 us)
Async XLA Ops:
  0.0 100.3 %copy-start = (s32[800]{0:T(1024)S(1)}, s32[800]{0:T(1024)}, u32[]{:S(2)}) copy-start(s32[800]{0:T(1024)} %param.8) | copy-start | bytes 9604
  39.2 56.2 %all-to-all-start = ((bf16[48,16,2500]{2,0,1:T(8,128)(2,1)}), bf16[48,16,2500]{2,0,1:T(8,128)(2,1)}, u32[]{:S(2)}, u32[]{:S(2)}) async-start(bf16[48,16,2500]{2,0,1:T(8,128)(2,1)} %bitcast.15), calls=%async_computation | async-start | bytes 7864320 | tf_op jit(solution)/shard_map/all_to_all | solution.py:40
  46.4 9.3 %copy-start.3 = (s32[384]{0:T(512)S(1)}, s32[384]{0:T(512)}, u32[]{:S(2)}) copy-start(s32[384]{0:T(512)} %param.9) | copy-start | bytes 4612
  95.4 78.0 %all-to-all-start.1 = ((bf16[48,16,2500]{2,0,1:T(8,128)(2,1)}), bf16[48,16,2500]{2,0,1:T(8,128)(2,1)}, u32[]{:S(2)}, u32[]{:S(2)}) async-start(bf16[48,16,2500]{2,0,1:T(8,128)(2,1)} %bitcast.14), calls=%async_computation.1 | async-start | bytes 7864320 | tf_op jit(solution)/shard_map/all_to_all | solution.py:40
  119.2 12.6 %copy-start.2 = (s32[120]{0:T(128)S(1)}, s32[120]{0:T(128)}, u32[]{:S(2)}) copy-start(s32[120]{0:T(128)} %param.7) | copy-start | bytes 1444
  173.4 132.5 %copy-start.1 = (s32[800]{0:T(1024)S(1)}, s32[800]{0:T(1024)}, u32[]{:S(2)}) copy-start(s32[800]{0:T(1024)} %param.8) | copy-start | bytes 9604

commit v4 on v2

v4 whole, which is shorter than its diff:
```python
import jax
import jax.numpy as jnp
from jax import lax
from jax.sharding import PartitionSpec as P

TR = 2
TILES_DEV = 3
CAP = 6
PIECES = 2


def lookup(table, index):
    levels = jnp.arange(1, 8, dtype=jnp.int32)
    starts = jnp.sum((table[None, :] < levels[:, None]).astype(jnp.int32), axis=1)
    return jnp.sum((index[:, None] >= starts[None, :]).astype(jnp.int32), axis=1)


def on_device(amplitudes, integrals, occ_irrep, vir_irrep, tile_owner):
    ncols = lax.axis_size("col")
    nrows = lax.axis_size("row")
    myself = lax.axis_index("row") * ncols + lax.axis_index("col")
    cd_dev = integrals.shape[0]
    ab_width = integrals.shape[1]
    local_pairs = amplitudes.shape[0]
    norb = occ_irrep.shape[0]
    nvirt = vir_irrep.shape[0]
    ab_index = jnp.arange(ab_width, dtype=jnp.int32)
    ab_irrep = jnp.bitwise_xor(
        lookup(vir_irrep, ab_index // nvirt), lookup(vir_irrep, ab_index % nvirt)
    )
    zero_half = jnp.zeros((), jnp.bfloat16)
    cd_index = myself * cd_dev + jnp.arange(cd_dev, dtype=jnp.int32)
    cd_irrep = jnp.bitwise_xor(
        lookup(vir_irrep, cd_index // nvirt), lookup(vir_irrep, cd_index % nvirt)
    )
    masked_v = jnp.where(cd_irrep[:, None] == ab_irrep[None, :], integrals, zero_half)
    rows_piece = local_pairs // PIECES
    terms = []
    for h in range(PIECES):
        part = amplitudes[h * rows_piece:(h + 1) * rows_piece]
        panel = lax.all_to_all(part, "col", split_axis=1, concat_axis=0, tiled=True)
        piece_pairs = (
            jnp.arange(ncols, dtype=jnp.int32)[:, None] * local_pairs
            + h * rows_piece
            + jnp.arange(rows_piece, dtype=jnp.int32)[None, :]
        ).reshape(ncols * rows_piece)
        piece_irrep = jnp.bitwise_xor(
            lookup(occ_irrep, piece_pairs // norb), lookup(occ_irrep, piece_pairs % norb)
        )
        masked_t = jnp.where(piece_irrep[:, None] == cd_irrep[None, :], panel, zero_half)
        terms.append(jnp.dot(masked_t, masked_v, preferred_element_type=jnp.float32))
    total = jnp.concatenate(terms, axis=0)
    ntiles = tile_owner.shape[0]
    tile_ids = jnp.arange(ntiles, dtype=jnp.int32)
    same = tile_owner[:, None] == tile_owner[None, :]
    earlier = tile_ids[:, None] > tile_ids[None, :]
    rank = jnp.sum(jnp.where(same & earlier, 1, 0), axis=1).astype(jnp.int32)
    slot = tile_owner * CAP + rank
    summed = lax.psum(total, ("row", "col"))
    wanted = myself * CAP + jnp.arange(CAP, dtype=jnp.int32)
    match = slot[None, :] == wanted[:, None]
    source = jnp.sum(jnp.where(match, tile_ids[None, :], 0), axis=1)
    found = jnp.any(match, axis=1)
    pair_rows = source[:, None] * TR + jnp.arange(TR, dtype=jnp.int32)[None, :]
    sender = pair_rows // local_pairs
    within = pair_rows % local_pairs
    which = (within // rows_piece).reshape(CAP * TR)
    rows = (sender * rows_piece + within % rows_piece).reshape(CAP * TR)
    keep = jnp.repeat(found, TR)
    flat_rows = which * (ncols * rows_piece) + rows
    summed = summed.reshape(PIECES * ncols * rows_piece, ab_width)
    picked = jnp.take(summed, flat_rows, axis=0).astype(jnp.bfloat16)
    placed = jnp.where(keep[:, None], picked, zero_half)
    return placed.reshape(CAP * TR, ab_width)


def solution(mesh):
    in_specs = (P("col", "row"), P(("row", "col"), None), P(), P(), P())
    out_specs = P(("row", "col"), None)
    return jax.shard_map(
        on_device, mesh=mesh, in_specs=in_specs, out_specs=out_specs, check_vma=False
    )
```

time: 264 us -> 261 us (0.989)
  waiting for transfers between devices: 83 us -> 66.4 us
  local copies, waits for them, and re-layouts: 32.4 us -> 42.7 us
  starting transfers between devices: 7.33 us -> 11.9 us
  other arithmetic: 8.4 us -> 5.26 us
    all_to_all x1 -> x2, waiting for transfers between devices: 83 us -> 66.4 us  [on_device(): panel = lax.all_to_all(part, 'col', split_axis=1, concat_axis=0, tiled=True)]
    reduce_sum x3 -> x5, other arithmetic: 6.99 us -> 0.76 us  [the longest x3 0.39 us: lookup(): jnp.sum((index[:, None] >= starts[None, :]).astype(jnp.int32), axis=1)]
    reshape x1 -> x0, local copies, waits for them, and re-layouts: 6.16 us -> none  [on_device(): every = summed.reshape(ntiles, TR * ab_width)]
    slice x0 -> x1, local copies, waits for them, and re-layouts: none -> 5.55 us  [on_device(): part = amplitudes[h * rows_piece:(h + 1) * rows_piece]]
    all_to_all x1 -> x2, starting transfers between devices: 7.33 us -> 11.9 us  [on_device(): panel = lax.all_to_all(part, 'col', split_axis=1, concat_axis=0, tiled=True)]
    all_to_all x2 -> x4, local copies, waits for them, and re-layouts: 25.2 us -> 29.3 us  [on_device(): panel = lax.all_to_all(part, 'col', split_axis=1, concat_axis=0, tiled=True)]
    psum x0 -> x1, local copies, waits for them, and re-layouts: none -> 3.98 us  [on_device(): summed = lax.psum(total, ('row', 'col'))]
    dot_general x1 -> x2, matrix products: 24.2 us -> 26.6 us  [on_device(): jnp.dot(masked_t, masked_v, preferred_element_type=jnp.float32)]
  transfers between devices with their start and end apart: 1 -> 2, of which waited for: 1 -> 2; matrix products, arithmetic and copies ran while one was open for 3% -> 9% of each run, Pallas kernels for 0% -> 0%
where the time goes in v4:
time: 261 us
  blocking collectives  108 us (41%)
  waiting for transfers between devices  66.4 us (25%)
  local copies, waits for them, and re-layouts  42.7 us (16%)
  matrix products  26.6 us (10%)
  starting transfers between devices  11.9 us (5%)
  other arithmetic  5.26 us (2%)
    psum x1, blocking collectives, on_device(): summed = lax.psum(total, ('row', 'col'))  108 us
    all_to_all x2, waiting for transfers between devices, on_device(): panel = lax.all_to_all(part, 'col', split_axis=1, concat_axis=0, tiled=True)  66.4 us
    all_to_all x4, local copies, waits for them, and re-layouts, on_device(): panel = lax.all_to_all(part, 'col', split_axis=1, concat_axis=0, tiled=True)  29.3 us
    dot_general x2, matrix products, on_device(): jnp.dot(masked_t, masked_v, preferred_element_type=jnp.float32)  26.6 us
    all_to_all x2, starting transfers between devices, on_device(): panel = lax.all_to_all(part, 'col', split_axis=1, concat_axis=0, tiled=True)  11.9 us
    slice x1, local copies, waits for them, and re-layouts, on_device(): part = amplitudes[h * rows_piece:(h + 1) * rows_piece]  5.55 us
  transfers between devices with their start and end apart: 2, of which 2 were waited for; matrix products, arithmetic and copies ran while one was open for 9% of the time, Pallas kernels for 0%

profile of v4, /device:TPU:0, one launch (start us, length us, event | category | flops | bytes accessed | tf_op | source)
XLA Modules:
  0.0 260.9 jit_solution(3675735086488277062)
XLA Ops:
  0.0 5.5 %fusion.36 = (bf16[24,80000]{1,0:T(8,128)(2,1)}, bf16[24,80000]{1,0:T(8,128)(2,1)}) fusion(bf16[48,80000]{1,0:T(8,128)(2,1)} %param.5), kind=kLoop, calls=%fused_computation.94 | loop fusion | bytes 15360000 | tf_op jit(solution)/shard_map/slice | solution.py:40
  5.5 8.4 %all_to_all.32 = bf16[24,16,5000]{2,1,0:T(8,128)(2,1)} reshape(bf16[24,80000]{1,0:T(8,128)(2,1)} %get-tuple-element.14) | data formatting | bytes 7680000 | tf_op jit(solution)/shard_map/all_to_all | solution.py:41
  14.0 6.2 %copy.11 = bf16[24,16,5000]{2,0,1:T(8,128)(2,1)} copy(bf16[24,16,5000]{2,1,0:T(8,128)(2,1)} %all_to_all.32) | data formatting | bytes 7680000 | tf_op jit(solution)/shard_map/all_to_all | solution.py:41
  20.2 7.2 %all-to-all-start.1 = ((bf16[24,16,5000]{2,0,1:T(8,128)(2,1)}), bf16[24,16,5000]{2,0,1:T(8,128)(2,1)}, u32[]{:S(2)}, u32[]{:S(2)}) async-start(bf16[24,16,5000]{2,0,1:T(8,128)(2,1)} %copy.11), calls=%async_computation.1 | async-start | bytes 7864320 | tf_op jit(solution)/shard_map/all_to_all | solution.py:41
  27.4 8.4 %all_to_all.28 = bf16[24,16,5000]{2,1,0:T(8,128)(2,1)} reshape(bf16[24,80000]{1,0:T(8,128)(2,1)} %get-tuple-element.13) | data formatting | bytes 7680000 | tf_op jit(solution)/shard_map/all_to_all | solution.py:41
  35.8 6.3 %copy.10 = bf16[24,16,5000]{2,0,1:T(8,128)(2,1)} copy(bf16[24,16,5000]{2,1,0:T(8,128)(2,1)} %all_to_all.28) | data formatting | bytes 7680000 | tf_op jit(solution)/shard_map/all_to_all | solution.py:41
  42.1 0.0 copy-done
  42.1 0.2 select_reduce_fusion
  42.3 0.2 fusion.19
  42.5 0.2 compare_reduce_fusion
  42.7 0.0 copy-done.1
  42.7 0.2 convert_reduce_fusion.4
  42.9 0.1 sign_compare_fusion.3
  43.0 0.1 sign_compare_fusion.1
  43.1 0.1 sign_compare_fusion.2
  43.1 0.1 fusion.27
  43.2 0.1 fusion.24
  43.3 0.1 fusion.25
  43.4 0.0 copy-start.2
  43.4 33.0 %all-to-all-done.1 = bf16[24,16,5000]{2,0,1:T(8,128)(2,1)} async-done(((bf16[24,16,5000]{2,0,1:T(8,128)(2,1)}), bf16[24,16,5000]{2,0,1:T(8,128)(2,1)}, u32[]{:S(2)}, u32[]{:S(2)}) %all-to-all-start.1) | async-done | bytes 3840032 | tf_op jit(solution)/shard_map/all_to_all | solution.py:41
  76.3 4.7 %all-to-all-start = ((bf16[24,16,5000]{2,0,1:T(8,128)(2,1)}), bf16[24,16,5000]{2,0,1:T(8,128)(2,1)}, u32[]{:S(2)}, u32[]{:S(2)}) async-start(bf16[24,16,5000]{2,0,1:T(8,128)(2,1)} %copy.10), calls=%async_computation | async-start | bytes 7864320 | tf_op jit(solution)/shard_map/all_to_all | solution.py:41
  81.1 0.1 rem.170
  81.2 0.1 rem.156
  81.3 0.1 div.92
  81.3 0.1 div.84
  81.4 0.1 ne.296
  81.5 0.1 ne.275
  81.6 0.1 rem.169
  81.7 0.1 div.90
  81.8 0.1 ne.290
  81.9 0.1 rem.162
  82.0 0.1 div.86
  82.1 0.1 ne.278
  82.2 0.1 broadcast_in_dim.44
  82.2 0.1 broadcast_in_dim.45
  82.3 0.2 convert_reduce_fusion
  82.5 0.1 convert_reduce_fusion.2
  82.7 0.0 copy-done.2
  82.7 0.2 convert_reduce_fusion.9
  82.9 0.1 convert_reduce_fusion.7
  83.1 13.3 %fusion = f32[384,1600]{0,1:T(8,128)S(1)} fusion(bf16[5000,1600]{0,1:T(8,128)(2,1)} %param.6, s32[5000]{0:T(1024)S(1)} %xor.33, s32[1600]{0:T(1024)S(1)} %xor.34, bf16[384,5000]{1,0:T(8,128)(2,1)} %bitcast.3, s32[384]{0:T(512)S(1)} %xor.35), kind=kOutput, calls=%fused_computation.5 | convolution fusion | flops 6163840000 | bytes 22325536 | tf_op jit(solution)/shard_map/dot_general | solution.py:51
  96.4 33.4 %all-to-all-done = bf16[24,16,5000]{2,0,1:T(8,128)(2,1)} async-done(((bf16[24,16,5000]{2,0,1:T(8,128)(2,1)}), bf16[24,16,5000]{2,0,1:T(8,128)(2,1)}, u32[]{:S(2)}, u32[]{:S(2)}) %all-to-all-start) | async-done | bytes 3840032 | tf_op jit(solution)/shard_map/all_to_all | solution.py:41
  129.8 13.3 %fusion.1 = f32[384,1600]{0,1:T(8,128)S(1)} fusion(bf16[5000,1600]{0,1:T(8,128)(2,1)} %param.6, s32[5000]{0:T(1024)S(1)} %xor.33, s32[1600]{0:T(1024)S(1)} %xor.34, bf16[384,5000]{1,0:T(8,128)(2,1)} %bitcast.1, s32[384]{0:T(512)S(1)} %xor.32), kind=kOutput, calls=%fused_computation.6 | convolution fusion | flops 6163840000 | bytes 22325536 | tf_op jit(solution)/shard_map/dot_general | solution.py:51
  143.1 2.6 pad_maximum_fusion
  145.7 107.8 %all-reduce.1 = bf16[768,1600]{0,1:T(8,128)(2,1)S(1)} all-reduce(f32[768,1600]{0,1:T(8,128)} %pad_maximum_fusion), channel_id=1, replica_groups=mesh['row'=8,'col'=16] {'row','col'}, use_global_device_ids=true, to_apply=%region_13.14 | all-reduce | flops 1228800 | bytes 7372800 | tf_op jit(solution)/shard_map/psum | solution.py:59
  253.5 4.0 %copy.12 = bf16[768,1600]{1,0:T(8,128)(2,1)} copy(bf16[768,1600]{0,1:T(8,128)(2,1)S(1)} %all-reduce.1) | data formatting | bytes 4915200 | tf_op jit(solution)/shard_map/psum | solution.py:59
  257.5 2.7 %gather_fusion = bf16[12,1600]{1,0:T(8,128)(2,1)S(1)} fusion(bf16[768,1600]{1,0:T(8,128)(2,1)} %copy.12, s32[1024]{0:T(1024)S(1)} %pad_clamp_fusion), kind=kCustom, calls=%fused_computation | custom fusion | bytes 76848 | tf_op jit(solution)/shard_map/jit(_take)/gather | solution.py:72
  260.2 0.7 fusion.9
  (18 shorter events, 0.1 us)
Async XLA Ops:
  20.2 56.2 %all-to-all-start.1 = ((bf16[24,16,5000]{2,0,1:T(8,128)(2,1)}), bf16[24,16,5000]{2,0,1:T(8,128)(2,1)}, u32[]{:S(2)}, u32[]{:S(2)}) async-start(bf16[24,16,5000]{2,0,1:T(8,128)(2,1)} %copy.11), calls=%async_computation.1 | async-start | bytes 7864320 | tf_op jit(solution)/shard_map/all_to_all | solution.py:41
  35.8 6.3 %copy-start = (s32[384]{0:T(512)S(1)}, s32[384]{0:T(512)}, u32[]{:S(2)}) copy-start(s32[384]{0:T(512)} %param.9) | copy-start | bytes 4612
  35.8 6.9 %copy-start.1 = (s32[800]{0:T(1024)S(1)}, s32[800]{0:T(1024)}, u32[]{:S(2)}) copy-start(s32[800]{0:T(1024)} %param.8) | copy-start | bytes 9604
  43.4 39.3 %copy-start.2 = (s32[120]{0:T(128)S(1)}, s32[120]{0:T(128)}, u32[]{:S(2)}) copy-start(s32[120]{0:T(128)} %param.7) | copy-start | bytes 1444
  76.3 53.5 %all-to-all-start = ((bf16[24,16,5000]{2,0,1:T(8,128)(2,1)}), bf16[24,16,5000]{2,0,1:T(8,128)(2,1)}, u32[]{:S(2)}, u32[]{:S(2)}) async-start(bf16[24,16,5000]{2,0,1:T(8,128)(2,1)} %copy.10), calls=%async_computation | async-start | bytes 7864320 | tf_op jit(solution)/shard_map/all_to_all | solution.py:41

commit v5 on v4

--- a/solution.py
+++ b/solution.py
@@ -48,15 +48,17 @@
             lookup(occ_irrep, piece_pairs // norb), lookup(occ_irrep, piece_pairs % norb)
         )
         masked_t = jnp.where(piece_irrep[:, None] == cd_irrep[None, :], panel, zero_half)
-        terms.append(jnp.dot(masked_t, masked_v, preferred_element_type=jnp.float32))
-    total = jnp.concatenate(terms, axis=0)
+        term = jnp.dot(masked_t, masked_v, preferred_element_type=jnp.float32)
+        if terms:
+            terms[-1], term = lax.optimization_barrier((terms[-1], term))
+        terms.append(lax.psum(term, ("row", "col")))
+    summed = jnp.concatenate(terms, axis=0)
     ntiles = tile_owner.shape[0]
     tile_ids = jnp.arange(ntiles, dtype=jnp.int32)
     same = tile_owner[:, None] == tile_owner[None, :]
     earlier = tile_ids[:, None] > tile_ids[None, :]
     rank = jnp.sum(jnp.where(same & earlier, 1, 0), axis=1).astype(jnp.int32)
     slot = tile_owner * CAP + rank
-    summed = lax.psum(total, ("row", "col"))
     wanted = myself * CAP + jnp.arange(CAP, dtype=jnp.int32)
     match = slot[None, :] == wanted[:, None]
     source = jnp.sum(jnp.where(match, tile_ids[None, :], 0), axis=1)

time: 261 us -> 347 us (1.33)
  blocking collectives: 108 us -> 229 us
  waiting for transfers between devices: 66.4 us -> 31.9 us
    psum x1 -> x2, blocking collectives: 108 us -> 229 us  [on_device(): terms.append(lax.psum(term, ('row', 'col')))]
    all_to_all x2, waiting for transfers between devices: 66.4 us -> 31.9 us  [on_device(): panel = lax.all_to_all(part, 'col', split_axis=1, concat_axis=0, tiled=True)]
    concatenate x0 -> x1, local copies, waits for them, and re-layouts: none -> 3.98 us  [on_device(): summed = jnp.concatenate(terms, axis=0)]
    psum x1 -> x0, local copies, waits for them, and re-layouts: 3.98 us -> none  [on_device(): summed = lax.psum(total, ('row', 'col'))]
  transfers between devices with their start and end apart: 2 -> 2, of which waited for: 2 -> 1; matrix products, arithmetic and copies ran while one was open for 9% -> 7% of each run, Pallas kernels for 0% -> 0%
where the time goes in v5:
time: 347 us; the launch traced here: 346 us
  blocking collectives  229 us (66%)
  local copies, waits for them, and re-layouts  42.7 us (12%)
  waiting for transfers between devices  31.9 us (9%)
  matrix products  26.6 us (8%)
  starting transfers between devices  11.9 us (3%)
  other arithmetic  4.54 us (1%)
    psum x2, blocking collectives, on_device(): terms.append(lax.psum(term, ('row', 'col')))  229 us
    all_to_all x2, waiting for transfers between devices, on_device(): panel = lax.all_to_all(part, 'col', split_axis=1, concat_axis=0, tiled=True)  31.9 us
    all_to_all x4, local copies, waits for them, and re-layouts, on_device(): panel = lax.all_to_all(part, 'col', split_axis=1, concat_axis=0, tiled=True)  29.3 us
    dot_general x2, matrix products, on_device(): term = jnp.dot(masked_t, masked_v, preferred_element_type=jnp.float32)  26.6 us
    all_to_all x2, starting transfers between devices, on_device(): panel = lax.all_to_all(part, 'col', split_axis=1, concat_axis=0, tiled=True)  11.9 us
  transfers between devices with their start and end apart: 2, of which 1 were waited for; matrix products, arithmetic and copies ran while one was open for 7% of the time, Pallas kernels for 0%

profile of v5, /device:TPU:0, one launch (start us, length us, event | category | flops | bytes accessed | tf_op | source)
XLA Modules:
  0.0 346.4 jit_solution(15701309858646907890)
XLA Ops:
  0.0 5.5 %fusion.36 = (bf16[24,80000]{1,0:T(8,128)(2,1)}, bf16[24,80000]{1,0:T(8,128)(2,1)}) fusion(bf16[48,80000]{1,0:T(8,128)(2,1)} %param.5), kind=kLoop, calls=%fused_computation.94 | loop fusion | bytes 15360000 | tf_op jit(solution)/shard_map/slice | solution.py:40
  5.5 8.4 %all_to_all.28 = bf16[24,16,5000]{2,1,0:T(8,128)(2,1)} reshape(bf16[24,80000]{1,0:T(8,128)(2,1)} %get-tuple-element.18) | data formatting | bytes 7680000 | tf_op jit(solution)/shard_map/all_to_all | solution.py:41
  14.0 6.2 %copy.10 = bf16[24,16,5000]{2,0,1:T(8,128)(2,1)} copy(bf16[24,16,5000]{2,1,0:T(8,128)(2,1)} %all_to_all.28) | data formatting | bytes 7680000 | tf_op jit(solution)/shard_map/all_to_all | solution.py:41
  20.2 7.2 %all-to-all-start = ((bf16[24,16,5000]{2,0,1:T(8,128)(2,1)}), bf16[24,16,5000]{2,0,1:T(8,128)(2,1)}, u32[]{:S(2)}, u32[]{:S(2)}) async-start(bf16[24,16,5000]{2,0,1:T(8,128)(2,1)} %copy.10), calls=%async_computation | async-start | bytes 7864320 | tf_op jit(solution)/shard_map/all_to_all | solution.py:41
  27.4 0.1 fusion.23
  27.4 0.1 div.90
  27.5 0.1 sign_compare_fusion.1
  27.6 0.1 ne.290
  27.7 0.1 rem.169
  27.8 0.1 fusion.25
  27.9 0.1 rem.162
  28.0 0.1 div.86
  28.1 0.1 sign_compare_fusion.2
  28.2 0.1 ne.278
  28.3 8.4 %all_to_all.32 = bf16[24,16,5000]{2,1,0:T(8,128)(2,1)} reshape(bf16[24,80000]{1,0:T(8,128)(2,1)} %get-tuple-element.17) | data formatting | bytes 7680000 | tf_op jit(solution)/shard_map/all_to_all | solution.py:41
  36.7 6.3 %copy.11 = bf16[24,16,5000]{2,0,1:T(8,128)(2,1)} copy(bf16[24,16,5000]{2,1,0:T(8,128)(2,1)} %all_to_all.32) | data formatting | bytes 7680000 | tf_op jit(solution)/shard_map/all_to_all | solution.py:41
  43.0 0.0 copy-done.2
  43.0 0.2 convert_reduce_fusion.9
  43.2 0.0 copy-done
  43.2 0.2 select_reduce_fusion
  43.5 0.2 fusion.19
  43.6 0.0 copy-done.1
  43.7 0.2 convert_reduce_fusion.4
  43.9 0.1 convert_reduce_fusion.5
  44.0 0.1 convert_reduce_fusion.2
  44.1 0.2 convert_reduce_fusion
  44.3 0.1 sign_compare_fusion.3
  44.3 0.1 fusion.27
  44.4 31.9 %all-to-all-done = bf16[24,16,5000]{2,0,1:T(8,128)(2,1)} async-done(((bf16[24,16,5000]{2,0,1:T(8,128)(2,1)}), bf16[24,16,5000]{2,0,1:T(8,128)(2,1)}, u32[]{:S(2)}, u32[]{:S(2)}) %all-to-all-start) | async-done | bytes 3840032 | tf_op jit(solution)/shard_map/all_to_all | solution.py:41
  76.3 4.7 %all-to-all-start.1 = ((bf16[24,16,5000]{2,0,1:T(8,128)(2,1)}), bf16[24,16,5000]{2,0,1:T(8,128)(2,1)}, u32[]{:S(2)}, u32[]{:S(2)}) async-start(bf16[24,16,5000]{2,0,1:T(8,128)(2,1)} %copy.11), calls=%async_computation.1 | async-start | bytes 7864320 | tf_op jit(solution)/shard_map/all_to_all | solution.py:41
  81.1 0.2 compare_reduce_fusion
  81.3 0.1 rem.170
  81.3 0.1 rem.156
  81.4 0.1 div.92
  81.5 0.1 div.84
  81.6 0.1 ne.296
  81.7 0.1 ne.275
  81.7 0.1 broadcast_in_dim.44
  81.8 0.1 broadcast_in_dim.45
  82.0 13.3 %fusion.1 = f32[384,1600]{0,1:T(8,128)S(1)} fusion(bf16[5000,1600]{0,1:T(8,128)(2,1)} %param.6, s32[5000]{0:T(1024)S(1)} %xor.33, s32[1600]{0:T(1024)S(1)} %xor.34, bf16[384,5000]{1,0:T(8,128)(2,1)} %bitcast.1, s32[384]{0:T(512)S(1)} %xor.32), kind=kOutput, calls=%fused_computation.6 | convolution fusion | flops 6163840000 | bytes 22325536 | tf_op jit(solution)/shard_map/dot_general | solution.py:51
  95.4 126.9 %all-reduce.2 = bf16[384,1600]{0,1:T(8,128)(2,1)} all-reduce(f32[384,1600]{0,1:T(8,128)S(1)} %fusion.1), channel_id=1, replica_groups=mesh['row'=8,'col'=16] {'row','col'}, use_global_device_ids=true, to_apply=%region_11.12 | all-reduce | flops 614400 | bytes 3686400 | tf_op jit(solution)/shard_map/psum | solution.py:54
  222.2 0.0 all-to-all-done.1
  222.2 13.3 %fusion = f32[384,1600]{0,1:T(8,128)S(1)} fusion(bf16[5000,1600]{0,1:T(8,128)(2,1)} %param.6, s32[5000]{0:T(1024)S(1)} %xor.33, s32[1600]{0:T(1024)S(1)} %xor.34, bf16[384,5000]{1,0:T(8,128)(2,1)} %bitcast.3, s32[384]{0:T(512)S(1)} %xor.35), kind=kOutput, calls=%fused_computation.5 | convolution fusion | flops 6163840000 | bytes 22325536 | tf_op jit(solution)/shard_map/dot_general | solution.py:51
  235.5 101.7 %all-reduce.3 = bf16[384,1600]{0,1:T(8,128)(2,1)} all-reduce(f32[384,1600]{0,1:T(8,128)S(1)} %fusion), channel_id=1, replica_groups=mesh['row'=8,'col'=16] {'row','col'}, use_global_device_ids=true, to_apply=%region_14.15 | all-reduce | flops 614400 | bytes 3686400 | tf_op jit(solution)/shard_map/psum | solution.py:54
  337.2 1.9 pad_maximum_fusion
  339.1 4.0 %copy.12 = bf16[768,1600]{1,0:T(8,128)(2,1)} copy(bf16[768,1600]{0,1:T(8,128)(2,1)S(1)} %pad_maximum_fusion) | data formatting | bytes 4915200 | tf_op jit(solution)/shard_map/concatenate | solution.py:55
  343.0 2.7 gather_fusion
  345.7 0.7 fusion.9
  (19 shorter events, 0.2 us)
Async XLA Ops:
  20.2 56.2 %all-to-all-start = ((bf16[24,16,5000]{2,0,1:T(8,128)(2,1)}), bf16[24,16,5000]{2,0,1:T(8,128)(2,1)}, u32[]{:S(2)}, u32[]{:S(2)}) async-start(bf16[24,16,5000]{2,0,1:T(8,128)(2,1)} %copy.10), calls=%async_computation | async-start | bytes 7864320 | tf_op jit(solution)/shard_map/all_to_all | solution.py:41
  36.7 6.4 %copy-start.2 = (s32[120]{0:T(128)S(1)}, s32[120]{0:T(128)}, u32[]{:S(2)}) copy-start(s32[120]{0:T(128)} %param.7) | copy-start | bytes 1444
  36.7 6.5 %copy-start = (s32[384]{0:T(512)S(1)}, s32[384]{0:T(512)}, u32[]{:S(2)}) copy-start(s32[384]{0:T(512)} %param.9) | copy-start | bytes 4612
  36.7 7.0 %copy-start.1 = (s32[800]{0:T(1024)S(1)}, s32[800]{0:T(1024)}, u32[]{:S(2)}) copy-start(s32[800]{0:T(1024)} %param.8) | copy-start | bytes 9604
  76.3 145.9 %all-to-all-start.1 = ((bf16[24,16,5000]{2,0,1:T(8,128)(2,1)}), bf16[24,16,5000]{2,0,1:T(8,128)(2,1)}, u32[]{:S(2)}, u32[]{:S(2)}) async-start(bf16[24,16,5000]{2,0,1:T(8,128)(2,1)} %copy.11), calls=%async_computation.1 | async-start | bytes 7864320 | tf_op jit(solution)/shard_map/all_to_all | solution.py:41

commit v6 on v4

--- a/solution.py
+++ b/solution.py
@@ -6,7 +6,7 @@
 TR = 2
 TILES_DEV = 3
 CAP = 6
-PIECES = 2
+PIECES = 3
 
 
 def lookup(table, index):
@@ -37,8 +37,12 @@
     rows_piece = local_pairs // PIECES
     terms = []
     for h in range(PIECES):
-        part = amplitudes[h * rows_piece:(h + 1) * rows_piece]
-        panel = lax.all_to_all(part, "col", split_axis=1, concat_axis=0, tiled=True)
+        part = jnp.transpose(
+            amplitudes[h * rows_piece:(h + 1) * rows_piece].reshape(rows_piece, ncols, cd_dev),
+            (1, 0, 2),
+        )
+        panel = lax.all_to_all(part, "col", split_axis=0, concat_axis=0, tiled=True)
+        panel = panel.reshape(ncols * rows_piece, cd_dev)
         piece_pairs = (
             jnp.arange(ncols, dtype=jnp.int32)[:, None] * local_pairs
             + h * rows_piece
@@ -69,7 +73,10 @@
     keep = jnp.repeat(found, TR)
     flat_rows = which * (ncols * rows_piece) + rows
     summed = summed.reshape(PIECES * ncols * rows_piece, ab_width)
-    picked = jnp.take(summed, flat_rows, axis=0).astype(jnp.bfloat16)
+    starts = flat_rows.reshape(CAP, TR)[:, 0]
+    picked = jnp.concatenate(
+        [lax.dynamic_slice_in_dim(summed, starts[k], TR, axis=0) for k in range(CAP)], axis=0
+    ).astype(jnp.bfloat16)
     placed = jnp.where(keep[:, None], picked, zero_half)
     return placed.reshape(CAP * TR, ab_width)
 

time: 261 us -> 261 us (level)
  waiting for transfers between devices: 66.4 us -> 46 us
  matrix products: 26.6 us -> 39.8 us
  between operations: 0.19 us -> 11.6 us
  local copies, waits for them, and re-layouts: 42.7 us -> 32.1 us
  starting transfers between devices: 11.9 us -> 15.7 us
    all_to_all x4 -> x0, local copies, waits for them, and re-layouts: 29.3 us -> none  [on_device(): panel = lax.all_to_all(part, 'col', split_axis=1, concat_axis=0, tiled=True)]
    reshape x0 -> x6, local copies, waits for them, and re-layouts: none -> 25 us  [on_device(): amplitudes[h * rows_piece:(h + 1) * rows_piece]]
    all_to_all x2 -> x3, waiting for transfers between devices: 66.4 us -> 46 us  [on_device(): panel = lax.all_to_all(part, 'col', split_axis=0, concat_axis=0, tiled=True)]
    dot_general x2 -> x3, matrix products: 26.6 us -> 39.8 us  [on_device(): jnp.dot(masked_t, masked_v, preferred_element_type=jnp.float32)]
    psum x1 -> x0, local copies, waits for them, and re-layouts: 3.98 us -> none  [on_device(): summed = lax.psum(total, ('row', 'col'))]
    all_to_all x2 -> x3, starting transfers between devices: 11.9 us -> 15.7 us  [on_device(): panel = lax.all_to_all(part, 'col', split_axis=0, concat_axis=0, tiled=True)]
    gather x1 -> x0, local copies, waits for them, and re-layouts: 2.68 us -> none  [on_device(): picked = jnp.take(summed, flat_rows, axis=0).astype(jnp.bfloat16)]
    slice x1 -> x2, local copies, waits for them, and re-layouts: 5.55 us -> 5.98 us  [the longest x1 5.38 us: on_device(): amplitudes[h * rows_piece:(h + 1) * rows_piece]]
  transfers between devices with their start and end apart: 2 -> 3, of which waited for: 2 -> 3; matrix products, arithmetic and copies ran while one was open for 9% -> 18% of each run, Pallas kernels for 0% -> 0%
where the time goes in v6:
time: 261 us; the launch traced here: 260 us
  blocking collectives  107 us (41%)
  waiting for transfers between devices  46 us (18%)
  matrix products  39.8 us (15%)
  local copies, waits for them, and re-layouts  32.1 us (12%)
  starting transfers between devices  15.7 us (6%)
  between operations  11.6 us (4%)
  other arithmetic  7.81 us (3%)
    psum x1, blocking collectives, on_device(): summed = lax.psum(total, ('row', 'col'))  107 us
    all_to_all x3, waiting for transfers between devices, on_device(): panel = lax.all_to_all(part, 'col', split_axis=0, concat_axis=0, tiled=True)  46 us
    dot_general x3, matrix products, on_device(): jnp.dot(masked_t, masked_v, preferred_element_type=jnp.float32)  39.8 us
    reshape x6, local copies, waits for them, and re-layouts, on_device(): amplitudes[h * rows_piece:(h + 1) * rows_piece]  25 us
    all_to_all x3, starting transfers between devices, on_device(): panel = lax.all_to_all(part, 'col', split_axis=0, concat_axis=0, tiled=True)  15.7 us
    slice x1, local copies, waits for them, and re-layouts, on_device(): amplitudes[h * rows_piece:(h + 1) * rows_piece]  5.38 us
  transfers between devices with their start and end apart: 3, of which 3 were waited for; matrix products, arithmetic and copies ran while one was open for 18% of the time, Pallas kernels for 0%

profile of v6, /device:TPU:0, one launch (start us, length us, event | category | flops | bytes accessed | tf_op | source)
XLA Modules:
  0.0 260.3 jit_solution(17274705334439424090)
XLA Ops:
  0.0 5.4 %fusion.49 = (bf16[16,80000]{1,0:T(8,128)(2,1)}, bf16[16,80000]{1,0:T(8,128)(2,1)}, bf16[16,80000]{1,0:T(8,128)(2,1)}) fusion(bf16[48,80000]{1,0:T(8,128)(2,1)} %param.5), kind=kLoop, calls=%fused_computation.120 | loop fusion | bytes 15360000 | tf_op jit(solution)/shard_map/slice | solution.py:41
  5.4 5.3 %reshape.253 = bf16[16,16,5000]{2,1,0:T(8,128)(2,1)S(1)} reshape(bf16[16,80000]{1,0:T(8,128)(2,1)} %get-tuple-element.16) | data formatting | bytes 5120000 | tf_op jit(solution)/shard_map/reshape | solution.py:41
  10.7 3.0 %copy.41 = bf16[16,16,5000]{2,0,1:T(8,128)(2,1)} copy(bf16[16,16,5000]{2,1,0:T(8,128)(2,1)S(1)} %reshape.253) | data formatting | bytes 5120000 | tf_op jit(solution)/shard_map/reshape | solution.py:41
  13.7 7.3 %all-to-all-start.2 = ((bf16[16,16,5000]{2,1,0:T(8,128)(2,1)}), bf16[16,16,5000]{2,1,0:T(8,128)(2,1)}, u32[]{:S(2)}, u32[]{:S(2)}) async-start(bf16[16,16,5000]{2,1,0:T(8,128)(2,1)} %bitcast.15), calls=%async_computation.2 | async-start | bytes 5242880 | tf_op jit(solution)/shard_map/all_to_all | solution.py:44
  21.1 0.2 select_reduce_fusion
  21.3 0.2 fusion.22
  21.5 0.1 fusion.33
  21.6 0.6 fusion.50
  29.8 0.1 fusion.30
  29.8 0.1 div.74
  29.9 0.1 sign_compare_fusion.3
  30.0 0.1 ne.230
  30.1 0.1 rem.150
  30.2 5.4 %reshape.251 = bf16[16,16,5000]{2,1,0:T(8,128)(2,1)S(1)} reshape(bf16[16,80000]{1,0:T(8,128)(2,1)} %get-tuple-element.17) | data formatting | bytes 5120000 | tf_op jit(solution)/shard_map/reshape | solution.py:41
  35.5 3.0 %copy.42 = bf16[16,16,5000]{2,0,1:T(8,128)(2,1)} copy(bf16[16,16,5000]{2,1,0:T(8,128)(2,1)S(1)} %reshape.251) | data formatting | bytes 5120000 | tf_op jit(solution)/shard_map/reshape | solution.py:41
  38.5 17.4 %all-to-all-done.2 = bf16[16,16,5000]{2,1,0:T(8,128)(2,1)} async-done(((bf16[16,16,5000]{2,1,0:T(8,128)(2,1)}), bf16[16,16,5000]{2,1,0:T(8,128)(2,1)}, u32[]{:S(2)}, u32[]{:S(2)}) %all-to-all-start.2) | async-done | bytes 2560032 | tf_op jit(solution)/shard_map/all_to_all | solution.py:44
  56.0 4.4 %all-to-all-start.1 = ((bf16[16,16,5000]{2,1,0:T(8,128)(2,1)}), bf16[16,16,5000]{2,1,0:T(8,128)(2,1)}, u32[]{:S(2)}, u32[]{:S(2)}) async-start(bf16[16,16,5000]{2,1,0:T(8,128)(2,1)} %bitcast.16), calls=%async_computation.1 | async-start | bytes 5242880 | tf_op jit(solution)/shard_map/all_to_all | solution.py:44
  60.4 0.1 fusion.27
  60.5 0.1 rem.159
  60.6 0.1 div.80
  60.7 0.1 sign_compare_fusion.1
  60.8 0.1 ne.245
  60.9 0.1 fusion.29
  60.9 0.1 div.78
  61.0 0.1 sign_compare_fusion.2
  61.1 0.1 ne.242
  61.2 0.1 rem.157
  61.3 5.4 %reshape.249 = bf16[16,16,5000]{2,1,0:T(8,128)(2,1)S(1)} reshape(bf16[16,80000]{1,0:T(8,128)(2,1)} %get-tuple-element.15) | data formatting | bytes 5120000 | tf_op jit(solution)/shard_map/reshape | solution.py:41
  66.7 2.9 %copy.43 = bf16[16,16,5000]{2,0,1:T(8,128)(2,1)} copy(bf16[16,16,5000]{2,1,0:T(8,128)(2,1)S(1)} %reshape.249) | data formatting | bytes 5120000 | tf_op jit(solution)/shard_map/reshape | solution.py:41
  69.6 0.2 compare_reduce_fusion
  69.8 0.1 broadcast_in_dim.38
  69.9 0.1 broadcast_in_dim.39
  70.0 0.2 convert_reduce_fusion.4
  70.2 0.2 convert_reduce_fusion
  70.4 0.2 convert_reduce_fusion.11
  70.6 0.1 convert_reduce_fusion.9
  70.7 0.1 convert_reduce_fusion.2
  74.7 20.7 %all-to-all-done.1 = bf16[16,16,5000]{2,1,0:T(8,128)(2,1)} async-done(((bf16[16,16,5000]{2,1,0:T(8,128)(2,1)}), bf16[16,16,5000]{2,1,0:T(8,128)(2,1)}, u32[]{:S(2)}, u32[]{:S(2)}) %all-to-all-start.1) | async-done | bytes 2560032 | tf_op jit(solution)/shard_map/all_to_all | solution.py:44
  95.4 3.9 %all-to-all-start = ((bf16[16,16,5000]{2,1,0:T(8,128)(2,1)}), bf16[16,16,5000]{2,1,0:T(8,128)(2,1)S(1)}, u32[]{:S(2)}, u32[]{:S(2)}) async-start(bf16[16,16,5000]{2,1,0:T(8,128)(2,1)} %bitcast.17), calls=%async_computation | async-start | bytes 5242880 | tf_op jit(solution)/shard_map/all_to_all | solution.py:44
  99.3 13.5 %fusion.2 = f32[256,1600]{1,0:T(8,128)} fusion(bf16[256,5000]{1,0:T(8,128)(2,1)} %bitcast.5, s32[5000]{0:T(1024)S(1)} %xor.40, s32[256]{0:T(256)S(1)} %xor.43, bf16[5000,1600]{0,1:T(8,128)(2,1)} %param.6, s32[1600]{0:T(1024)S(1)} %xor.41), kind=kOutput, calls=%fused_computation.7 | convolution fusion | flops 4114560000 | bytes 20225824 | tf_op jit(solution)/shard_map/dot_general | solution.py:55
  112.8 13.4 %fusion.1 = f32[256,1600]{1,0:T(8,128)} fusion(bf16[256,5000]{1,0:T(8,128)(2,1)} %bitcast.3, s32[5000]{0:T(1024)S(1)} %xor.40, s32[256]{0:T(256)S(1)} %xor.42, bf16[5000,1600]{0,1:T(8,128)(2,1)} %param.6, s32[1600]{0:T(1024)S(1)} %xor.41), kind=kOutput, calls=%fused_computation.6 | convolution fusion | flops 4114560000 | bytes 20225824 | tf_op jit(solution)/shard_map/dot_general | solution.py:55
  126.2 7.8 %all-to-all-done = bf16[16,16,5000]{2,1,0:T(8,128)(2,1)S(1)} async-done(((bf16[16,16,5000]{2,1,0:T(8,128)(2,1)}), bf16[16,16,5000]{2,1,0:T(8,128)(2,1)S(1)}, u32[]{:S(2)}, u32[]{:S(2)}) %all-to-all-start) | async-done | bytes 2560032 | tf_op jit(solution)/shard_map/all_to_all | solution.py:44
  134.0 12.9 %fusion = f32[256,1600]{1,0:T(8,128)} fusion(bf16[256,5000]{1,0:T(8,128)(2,1)S(1)} %bitcast.18, s32[5000]{0:T(1024)S(1)} %xor.40, s32[256]{0:T(256)S(1)} %xor.39, bf16[5000,1600]{0,1:T(8,128)(2,1)} %param.6, s32[1600]{0:T(1024)S(1)} %xor.41), kind=kOutput, calls=%fused_computation.5 | convolution fusion | flops 4114560000 | bytes 20225824 | tf_op jit(solution)/shard_map/dot_general | solution.py:55
  146.9 5.1 %pad_maximum_fusion = f32[768,1600]{1,0:T(8,128)} fusion(f32[256,1600]{1,0:T(8,128)} %fusion.2, f32[256,1600]{1,0:T(8,128)} %fusion.1, f32[256,1600]{1,0:T(8,128)} %fusion), kind=kLoop, calls=%fused_computation.4 | loop fusion | flops 2457600 | bytes 9830400 | tf_op jit(solution)/shard_map/concatenate | solution.py:56
  152.0 107.4 %all-reduce.1 = bf16[768,1600]{1,0:T(8,128)(2,1)S(1)} all-reduce(f32[768,1600]{1,0:T(8,128)} %pad_maximum_fusion), channel_id=1, replica_groups=mesh['row'=8,'col'=16] {'row','col'}, use_global_device_ids=true, to_apply=%region_14.15 | all-reduce | flops 1228800 | bytes 7372800 | tf_op jit(solution)/shard_map/psum | solution.py:63
  259.4 0.1 dynamic-slice_convert_fusion
  259.5 0.1 concatenate.8
  259.6 0.7 broadcast_select_fusion
  (22 shorter events, 0.1 us)
Async XLA Ops:
  13.7 7.4 %copy-start = (s32[384]{0:T(512)S(1)}, s32[384]{0:T(512)}, u32[]{:S(2)}) copy-start(s32[384]{0:T(512)} %param.9) | copy-start | bytes 4612
  13.7 42.3 %all-to-all-start.2 = ((bf16[16,16,5000]{2,1,0:T(8,128)(2,1)}), bf16[16,16,5000]{2,1,0:T(8,128)(2,1)}, u32[]{:S(2)}, u32[]{:S(2)}) async-start(bf16[16,16,5000]{2,1,0:T(8,128)(2,1)} %bitcast.15), calls=%async_computation.2 | async-start | bytes 5242880 | tf_op jit(solution)/shard_map/all_to_all | solution.py:44
  56.0 39.4 %all-to-all-start.1 = ((bf16[16,16,5000]{2,1,0:T(8,128)(2,1)}), bf16[16,16,5000]{2,1,0:T(8,128)(2,1)}, u32[]{:S(2)}, u32[]{:S(2)}) async-start(bf16[16,16,5000]{2,1,0:T(8,128)(2,1)} %bitcast.16), calls=%async_computation.1 | async-start | bytes 5242880 | tf_op jit(solution)/shard_map/all_to_all | solution.py:44
  66.6 3.4 %copy-start.1 = (s32[800]{0:T(1024)S(1)}, s32[800]{0:T(1024)}, u32[]{:S(2)}) copy-start(s32[800]{0:T(1024)} %param.8) | copy-start | bytes 9604
  66.6 3.7 %copy-start.2 = (s32[120]{0:T(128)S(1)}, s32[120]{0:T(128)}, u32[]{:S(2)}) copy-start(s32[120]{0:T(128)} %param.7) | copy-start | bytes 1444
  95.4 38.6 %all-to-all-start = ((bf16[16,16,5000]{2,1,0:T(8,128)(2,1)}), bf16[16,16,5000]{2,1,0:T(8,128)(2,1)S(1)}, u32[]{:S(2)}, u32[]{:S(2)}) async-start(bf16[16,16,5000]{2,1,0:T(8,128)(2,1)} %bitcast.17), calls=%async_computation | async-start | bytes 5242880 | tf_op jit(solution)/shard_map/all_to_all | solution.py:44

commit v7 on v6

--- a/solution.py
+++ b/solution.py
@@ -6,7 +6,7 @@
 TR = 2
 TILES_DEV = 3
 CAP = 6
-PIECES = 3
+PIECES = 2
 
 
 def lookup(table, index):
@@ -36,9 +36,10 @@
     masked_v = jnp.where(cd_irrep[:, None] == ab_irrep[None, :], integrals, zero_half)
     rows_piece = local_pairs // PIECES
     terms = []
+    stacked = amplitudes.reshape(PIECES, rows_piece, ncols * cd_dev)
     for h in range(PIECES):
         part = jnp.transpose(
-            amplitudes[h * rows_piece:(h + 1) * rows_piece].reshape(rows_piece, ncols, cd_dev),
+            stacked[h].reshape(rows_piece, ncols, cd_dev),
             (1, 0, 2),
         )
         panel = lax.all_to_all(part, "col", split_axis=0, concat_axis=0, tiled=True)

time: 261 us -> 259 us (level)
  matrix products: 39.8 us -> 30.2 us
  waiting for transfers between devices: 46 us -> 53.8 us
  local copies, waits for them, and re-layouts: 32.1 us -> 36.3 us
  starting transfers between devices: 15.7 us -> 12.2 us
    another operation x1 -> x5, local copies, waits for them, and re-layouts: 0.09 us -> 29.4 us  [the longest x4 29.3 us: on_device(): stacked[h].reshape(rows_piece, ncols, cd_dev)]
    reshape x6 -> x0, local copies, waits for them, and re-layouts: 25 us -> none  [on_device(): amplitudes[h * rows_piece:(h + 1) * rows_piece]]
    dot_general x3 -> x2, matrix products: 39.8 us -> 30.2 us  [on_device(): jnp.dot(masked_t, masked_v, preferred_element_type=jnp.float32)]
    all_to_all x3 -> x2, waiting for transfers between devices: 46 us -> 53.8 us  [on_device(): panel = lax.all_to_all(part, 'col', split_axis=0, concat_axis=0, tiled=True)]
    all_to_all x3 -> x2, starting transfers between devices: 15.7 us -> 12.2 us  [on_device(): panel = lax.all_to_all(part, 'col', split_axis=0, concat_axis=0, tiled=True)]
  transfers between devices with their start and end apart: 3 -> 2, of which waited for: 3 -> 2; matrix products, arithmetic and copies ran while one was open for 18% -> 13% of each run, Pallas kernels for 0% -> 0%
where the time goes in v7:
time: 259 us; the launch traced here: 258 us
  blocking collectives  107 us (41%)
  waiting for transfers between devices  53.8 us (21%)
  local copies, waits for them, and re-layouts  36.3 us (14%)
  matrix products  30.2 us (12%)
  starting transfers between devices  12.2 us (5%)
  between operations  11.6 us (4%)
  other arithmetic  6.88 us (3%)
    psum x1, blocking collectives, on_device(): summed = lax.psum(total, ('row', 'col'))  107 us
    all_to_all x2, waiting for transfers between devices, on_device(): panel = lax.all_to_all(part, 'col', split_axis=0, concat_axis=0, tiled=True)  53.8 us
    dot_general x2, matrix products, on_device(): jnp.dot(masked_t, masked_v, preferred_element_type=jnp.float32)  30.2 us
    another operation x4, local copies, waits for them, and re-layouts, on_device(): stacked[h].reshape(rows_piece, ncols, cd_dev)  29.3 us
    all_to_all x2, starting transfers between devices, on_device(): panel = lax.all_to_all(part, 'col', split_axis=0, concat_axis=0, tiled=True)  12.2 us
    slice x1, local copies, waits for them, and re-layouts, on_device(): stacked[h].reshape(rows_piece, ncols, cd_dev)  5.55 us
  transfers between devices with their start and end apart: 2, of which 2 were waited for; matrix products, arithmetic and copies ran while one was open for 13% of the time, Pallas kernels for 0%

profile of v7, /device:TPU:0, one launch (start us, length us, event | category | flops | bytes accessed | tf_op | source)
XLA Modules:
  0.0 258.4 jit_solution(6360994347540456638)
XLA Ops:
  0.0 5.5 %fusion.42 = (bf16[24,80000]{1,0:T(8,128)(2,1)}, bf16[24,80000]{1,0:T(8,128)(2,1)}) fusion(bf16[48,80000]{1,0:T(8,128)(2,1)} %param.5), kind=kLoop, calls=%fused_computation.100 | loop fusion | bytes 15360000 | tf_op jit(solution)/shard_map/slice | solution.py:42
  5.5 8.4 %reshape_squeeze.7 = bf16[24,16,5000]{2,1,0:T(8,128)(2,1)} reshape(bf16[24,80000]{1,0:T(8,128)(2,1)} %get-tuple-element.14) | data formatting | bytes 7680000 | tf_op jit(solution)/shard_map/reshape;squeeze | solution.py:42
  14.0 6.2 %copy.34 = bf16[24,16,5000]{2,0,1:T(8,128)(2,1)} copy(bf16[24,16,5000]{2,1,0:T(8,128)(2,1)} %reshape_squeeze.7) | data formatting | bytes 7680000 | tf_op jit(solution)/shard_map/reshape;squeeze | solution.py:42
  20.2 0.0 copy-start
  20.2 7.3 %all-to-all-start.1 = ((bf16[16,24,5000]{2,1,0:T(8,128)(2,1)}), bf16[16,24,5000]{2,1,0:T(8,128)(2,1)}, u32[]{:S(2)}, u32[]{:S(2)}) async-start(bf16[16,24,5000]{2,1,0:T(8,128)(2,1)} %bitcast.15), calls=%async_computation.1 | async-start | bytes 7864320 | tf_op jit(solution)/shard_map/all_to_all | solution.py:45
  27.5 0.0 copy-done
  27.5 0.2 select_reduce_fusion
  27.8 0.2 fusion.18
  27.9 0.1 fusion.27
  28.0 0.6 fusion.43
  36.3 0.1 fusion.23
  36.3 0.1 rem.127
  36.4 0.1 div.63
  36.5 0.1 sign_compare_fusion.1
  36.6 0.1 ne.211
  36.7 0.1 fusion.24
  36.8 0.1 rem.120
  36.9 0.1 div.59
  37.0 8.4 %reshape_squeeze.6 = bf16[24,16,5000]{2,1,0:T(8,128)(2,1)} reshape(bf16[24,80000]{1,0:T(8,128)(2,1)} %get-tuple-element.13) | data formatting | bytes 7680000 | tf_op jit(solution)/shard_map/reshape;squeeze | solution.py:42
  45.4 6.3 %copy.35 = bf16[24,16,5000]{2,0,1:T(8,128)(2,1)} copy(bf16[24,16,5000]{2,1,0:T(8,128)(2,1)} %reshape_squeeze.6) | data formatting | bytes 7680000 | tf_op jit(solution)/shard_map/reshape;squeeze | solution.py:42
  51.6 24.8 %all-to-all-done.1 = bf16[16,24,5000]{2,1,0:T(8,128)(2,1)} async-done(((bf16[16,24,5000]{2,1,0:T(8,128)(2,1)}), bf16[16,24,5000]{2,1,0:T(8,128)(2,1)}, u32[]{:S(2)}, u32[]{:S(2)}) %all-to-all-start.1) | async-done | bytes 3840032 | tf_op jit(solution)/shard_map/all_to_all | solution.py:45
  76.5 0.0 copy-start.1
  76.5 0.0 copy-start.2
  76.5 4.9 %all-to-all-start = ((bf16[16,24,5000]{2,1,0:T(8,128)(2,1)}), bf16[16,24,5000]{2,1,0:T(8,128)(2,1)}, u32[]{:S(2)}, u32[]{:S(2)}) async-start(bf16[16,24,5000]{2,1,0:T(8,128)(2,1)} %bitcast.14), calls=%async_computation | async-start | bytes 7864320 | tf_op jit(solution)/shard_map/all_to_all | solution.py:45
  81.3 0.1 sign_compare_fusion.2
  81.4 0.1 ne.199
  81.5 0.2 compare_reduce_fusion
  81.7 0.1 broadcast_in_dim.37
  81.8 0.1 broadcast_in_dim.38
  81.9 0.0 copy-done.1
  81.9 0.2 convert_reduce_fusion.4
  82.1 0.2 convert_reduce_fusion
  82.3 0.1 convert_reduce_fusion.2
  82.5 0.0 copy-done.2
  82.5 0.2 convert_reduce_fusion.9
  82.7 0.1 convert_reduce_fusion.7
  86.6 14.6 %fusion = f32[384,1600]{1,0:T(8,128)S(1)} fusion(bf16[5000,1600]{0,1:T(8,128)(2,1)} %param.6, s32[5000]{0:T(1024)S(1)} %xor.33, s32[1600]{0:T(1024)S(1)} %xor.34, bf16[384,5000]{1,0:T(8,128)(2,1)} %bitcast.3, s32[384]{0:T(512)S(1)} %xor.35), kind=kOutput, calls=%fused_computation.4 | convolution fusion | flops 6163840000 | bytes 22325536 | tf_op jit(solution)/shard_map/dot_general | solution.py:56
  101.2 28.9 %all-to-all-done = bf16[16,24,5000]{2,1,0:T(8,128)(2,1)} async-done(((bf16[16,24,5000]{2,1,0:T(8,128)(2,1)}), bf16[16,24,5000]{2,1,0:T(8,128)(2,1)}, u32[]{:S(2)}, u32[]{:S(2)}) %all-to-all-start) | async-done | bytes 3840032 | tf_op jit(solution)/shard_map/all_to_all | solution.py:45
  130.1 15.6 %fusion.1 = f32[384,1600]{1,0:T(8,128)} fusion(bf16[5000,1600]{0,1:T(8,128)(2,1)} %param.6, s32[5000]{0:T(1024)S(1)} %xor.33, s32[1600]{0:T(1024)S(1)} %xor.34, bf16[384,5000]{1,0:T(8,128)(2,1)} %bitcast.1, s32[384]{0:T(512)S(1)} %xor.32), kind=kOutput, calls=%fused_computation.5 | convolution fusion | flops 6163840000 | bytes 22325536 | tf_op jit(solution)/shard_map/dot_general | solution.py:56
  145.7 4.3 %pad_maximum_fusion = f32[768,1600]{1,0:T(8,128)} fusion(f32[384,1600]{1,0:T(8,128)S(1)} %fusion, f32[384,1600]{1,0:T(8,128)} %fusion.1), kind=kLoop, calls=%fused_computation.3 | loop fusion | flops 1228800 | bytes 9830400 | tf_op jit(solution)/shard_map/concatenate | solution.py:57
  150.0 107.4 %all-reduce.1 = bf16[768,1600]{1,0:T(8,128)(2,1)S(1)} all-reduce(f32[768,1600]{1,0:T(8,128)} %pad_maximum_fusion), channel_id=1, replica_groups=mesh['row'=8,'col'=16] {'row','col'}, use_global_device_ids=true, to_apply=%region_12.13 | all-reduce | flops 1228800 | bytes 7372800 | tf_op jit(solution)/shard_map/psum | solution.py:64
  257.5 0.1 dynamic-slice_convert_fusion
  257.6 0.1 concatenate.8
  257.7 0.7 broadcast_select_fusion
  (13 shorter events, 0.1 us)
Async XLA Ops:
  20.2 7.4 %copy-start = (s32[384]{0:T(512)S(1)}, s32[384]{0:T(512)}, u32[]{:S(2)}) copy-start(s32[384]{0:T(512)} %param.9) | copy-start | bytes 4612
  20.2 56.3 %all-to-all-start.1 = ((bf16[16,24,5000]{2,1,0:T(8,128)(2,1)}), bf16[16,24,5000]{2,1,0:T(8,128)(2,1)}, u32[]{:S(2)}, u32[]{:S(2)}) async-start(bf16[16,24,5000]{2,1,0:T(8,128)(2,1)} %bitcast.15), calls=%async_computation.1 | async-start | bytes 7864320 | tf_op jit(solution)/shard_map/all_to_all | solution.py:45
  76.5 5.4 %copy-start.1 = (s32[800]{0:T(1024)S(1)}, s32[800]{0:T(1024)}, u32[]{:S(2)}) copy-start(s32[800]{0:T(1024)} %param.8) | copy-start | bytes 9604
  76.5 6.0 %copy-start.2 = (s32[120]{0:T(128)S(1)}, s32[120]{0:T(128)}, u32[]{:S(2)}) copy-start(s32[120]{0:T(128)} %param.7) | copy-start | bytes 1444
  76.5 53.6 %all-to-all-start = ((bf16[16,24,5000]{2,1,0:T(8,128)(2,1)}), bf16[16,24,5000]{2,1,0:T(8,128)(2,1)}, u32[]{:S(2)}, u32[]{:S(2)}) async-start(bf16[16,24,5000]{2,1,0:T(8,128)(2,1)} %bitcast.14), calls=%async_computation | async-start | bytes 7864320 | tf_op jit(solution)/shard_map/all_to_all | solution.py:45

commit v8 on v6

--- a/solution.py
+++ b/solution.py
@@ -6,7 +6,7 @@
 TR = 2
 TILES_DEV = 3
 CAP = 6
-PIECES = 3
+FIRST_ROWS = 8
 
 
 def lookup(table, index):
@@ -34,18 +34,19 @@
         lookup(vir_irrep, cd_index // nvirt), lookup(vir_irrep, cd_index % nvirt)
     )
     masked_v = jnp.where(cd_irrep[:, None] == ab_irrep[None, :], integrals, zero_half)
-    rows_piece = local_pairs // PIECES
+    cuts = [0, FIRST_ROWS, local_pairs]
     terms = []
-    for h in range(PIECES):
+    for h in range(len(cuts) - 1):
+        lo, rows_piece = cuts[h], cuts[h + 1] - cuts[h]
         part = jnp.transpose(
-            amplitudes[h * rows_piece:(h + 1) * rows_piece].reshape(rows_piece, ncols, cd_dev),
+            amplitudes[lo:lo + rows_piece].reshape(rows_piece, ncols, cd_dev),
             (1, 0, 2),
         )
         panel = lax.all_to_all(part, "col", split_axis=0, concat_axis=0, tiled=True)
         panel = panel.reshape(ncols * rows_piece, cd_dev)
         piece_pairs = (
             jnp.arange(ncols, dtype=jnp.int32)[:, None] * local_pairs
-            + h * rows_piece
+            + lo
             + jnp.arange(rows_piece, dtype=jnp.int32)[None, :]
         ).reshape(ncols * rows_piece)
         piece_irrep = jnp.bitwise_xor(
@@ -68,11 +69,13 @@
     pair_rows = source[:, None] * TR + jnp.arange(TR, dtype=jnp.int32)[None, :]
     sender = pair_rows // local_pairs
     within = pair_rows % local_pairs
-    which = (within // rows_piece).reshape(CAP * TR)
-    rows = (sender * rows_piece + within % rows_piece).reshape(CAP * TR)
+    late = within >= FIRST_ROWS
+    flat_rows = jnp.where(
+        late,
+        ncols * FIRST_ROWS + sender * (local_pairs - FIRST_ROWS) + within - FIRST_ROWS,
+        sender * FIRST_ROWS + within,
+    ).reshape(CAP * TR)
     keep = jnp.repeat(found, TR)
-    flat_rows = which * (ncols * rows_piece) + rows
-    summed = summed.reshape(PIECES * ncols * rows_piece, ab_width)
     starts = flat_rows.reshape(CAP, TR)[:, 0]
     picked = jnp.concatenate(
         [lax.dynamic_slice_in_dim(summed, starts[k], TR, axis=0) for k in range(CAP)], axis=0

time: 261 us -> 262 us (level)
  waiting for transfers between devices: 46 us -> 52 us
  matrix products: 39.8 us -> 34.7 us
  local copies, waits for them, and re-layouts: 32.1 us -> 36.4 us
    all_to_all x3 -> x2, waiting for transfers between devices: 46 us -> 52 us  [on_device(): panel = lax.all_to_all(part, 'col', split_axis=0, concat_axis=0, tiled=True)]
    dot_general x3 -> x2, matrix products: 39.8 us -> 34.7 us  [on_device(): jnp.dot(masked_t, masked_v, preferred_element_type=jnp.float32)]
    slice x1 -> x2, local copies, waits for them, and re-layouts: 5.38 us -> 7.3 us  [on_device(): amplitudes[lo:lo + rows_piece].reshape(rows_piece, ncols, cd_dev)]
    all_to_all x3 -> x2, starting transfers between devices: 15.7 us -> 14.6 us  [on_device(): panel = lax.all_to_all(part, 'col', split_axis=0, concat_axis=0, tiled=True)]
    reshape x6 -> x4, local copies, waits for them, and re-layouts: 25 us -> 25.7 us  [on_device(): amplitudes[lo:lo + rows_piece].reshape(rows_piece, ncols, cd_dev)]
  transfers between devices with their start and end apart: 3 -> 2, of which waited for: 3 -> 1; matrix products, arithmetic and copies ran while one was open for 18% -> 16% of each run, Pallas kernels for 0% -> 0%
where the time goes in v8:
time: 262 us
  blocking collectives  107 us (41%)
  waiting for transfers between devices  52 us (20%)
  local copies, waits for them, and re-layouts  36.4 us (14%)
  matrix products  34.7 us (13%)
  starting transfers between devices  14.6 us (6%)
  between operations  11.5 us (4%)
  other arithmetic  5.24 us (2%)
    psum x1, blocking collectives, on_device(): summed = lax.psum(total, ('row', 'col'))  107 us
    all_to_all x2, waiting for transfers between devices, on_device(): panel = lax.all_to_all(part, 'col', split_axis=0, concat_axis=0, tiled=True)  52 us
    dot_general x2, matrix products, on_device(): jnp.dot(masked_t, masked_v, preferred_element_type=jnp.float32)  34.7 us
    reshape x4, local copies, waits for them, and re-layouts, on_device(): amplitudes[lo:lo + rows_piece].reshape(rows_piece, ncols, cd_dev)  25.7 us
    all_to_all x2, starting transfers between devices, on_device(): panel = lax.all_to_all(part, 'col', split_axis=0, concat_axis=0, tiled=True)  14.6 us
    slice x2, local copies, waits for them, and re-layouts, on_device(): amplitudes[lo:lo + rows_piece].reshape(rows_piece, ncols, cd_dev)  7.3 us
  transfers between devices with their start and end apart: 2, of which 1 were waited for; matrix products, arithmetic and copies ran while one was open for 16% of the time, Pallas kernels for 0%

profile of v8, /device:TPU:0, one launch (start us, length us, event | category | flops | bytes accessed | tf_op | source)
XLA Modules:
  0.0 261.8 jit_solution(3937548009675588354)
XLA Ops:
  0.0 1.4 slice.37
  1.4 1.9 reshape.194
  3.3 2.2 reshape.190
  5.5 1.8 copy.35
  7.3 7.1 %all-to-all-start = ((bf16[16,8,5000]{2,1,0:T(8,128)(2,1)}), bf16[16,8,5000]{2,1,0:T(8,128)(2,1)S(1)}, u32[]{:S(2)}, u32[]{:S(2)}) async-start(bf16[16,8,5000]{2,1,0:T(8,128)(2,1)} %bitcast.17), calls=%async_computation | async-start | bytes 2621440 | tf_op jit(solution)/shard_map/all_to_all | solution.py:45
  14.5 5.9 %slice.38 = bf16[40,80000]{1,0:T(8,128)(2,1)} slice(bf16[48,80000]{1,0:T(8,128)(2,1)} %param.5), slice={[8:48], [0:80000]} | slice | bytes 12800000 | tf_op jit(solution)/shard_map/slice | solution.py:42
  20.4 12.5 %reshape.192 = bf16[40,16,5000]{2,1,0:T(8,128)(2,1)} reshape(bf16[40,80000]{1,0:T(8,128)(2,1)} %slice.38) | data formatting | bytes 12800000 | tf_op jit(solution)/shard_map/reshape | solution.py:42
  32.9 9.2 %copy.34 = bf16[40,16,5000]{2,0,1:T(8,128)(2,1)} copy(bf16[40,16,5000]{2,1,0:T(8,128)(2,1)} %reshape.192) | data formatting | bytes 12800000 | tf_op jit(solution)/shard_map/reshape | solution.py:42
  42.0 0.0 all-to-all-done
  42.1 0.0 copy-start
  42.1 0.0 copy-start.1
  42.1 0.0 copy-start.2
  42.1 7.4 %all-to-all-start.1 = ((bf16[16,40,5000]{2,1,0:T(8,128)(2,1)}), bf16[16,40,5000]{2,1,0:T(8,128)(2,1)}, u32[]{:S(2)}, u32[]{:S(2)}) async-start(bf16[16,40,5000]{2,1,0:T(8,128)(2,1)} %bitcast.18), calls=%async_computation.1 | async-start | bytes 13107200 | tf_op jit(solution)/shard_map/all_to_all | solution.py:45
  49.5 0.0 copy-done
  49.5 0.2 select_reduce_fusion
  49.8 0.2 fusion.19
  49.9 0.1 add_select_fusion.7
  50.0 0.6 fusion.35
  58.2 0.1 fusion.23
  58.3 0.1 div.57
  58.3 0.1 sign_compare_fusion.1
  58.4 0.1 ne.193
  58.5 0.1 rem.118
  58.6 0.1 fusion.25
  58.7 0.1 div.53
  58.8 0.1 sign_compare_fusion.2
  58.9 0.1 ne.180
  59.0 0.1 rem.110
  59.1 0.2 compare_reduce_fusion
  59.3 0.1 broadcast_in_dim.39
  59.3 0.1 broadcast_in_dim.40
  59.5 0.0 copy-done.1
  59.5 0.2 convert_reduce_fusion.4
  59.7 0.2 convert_reduce_fusion
  59.9 0.0 copy-done.2
  59.9 0.2 convert_reduce_fusion.9
  60.1 0.1 convert_reduce_fusion.5
  60.2 0.1 convert_reduce_fusion.2
  60.3 0.1 convert_reduce_fusion.7
  64.2 10.4 %fusion.3 = f32[128,1600]{1,0:T(8,128)S(1)} fusion(bf16[5000,1600]{0,1:T(8,128)(2,1)} %param.6, s32[5000]{0:T(1024)S(1)} %xor.33, s32[1600]{0:T(1024)S(1)} %xor.34, bf16[16,8,5000]{2,1,0:T(8,128)(2,1)S(1)} %all-to-all-done, s32[128]{0:T(128)S(1)} %xor.32), kind=kOutput, calls=%fused_computation.7 | convolution fusion | flops 2065280000 | bytes 18126112 | tf_op jit(solution)/shard_map/dot_general | solution.py:56
  74.6 52.0 %all-to-all-done.1 = bf16[16,40,5000]{2,1,0:T(8,128)(2,1)} async-done(((bf16[16,40,5000]{2,1,0:T(8,128)(2,1)}), bf16[16,40,5000]{2,1,0:T(8,128)(2,1)}, u32[]{:S(2)}, u32[]{:S(2)}) %all-to-all-start.1) | async-done | bytes 6400032 | tf_op jit(solution)/shard_map/all_to_all | solution.py:45
  126.6 24.3 %fusion = f32[640,1600]{1,0:T(8,128)S(1)} fusion(bf16[640,5000]{1,0:T(8,128)(2,1)} %bitcast.3, s32[5000]{0:T(1024)S(1)} %xor.33, s32[640]{0:T(1024)S(1)} %xor.35, bf16[5000,1600]{0,1:T(8,128)(2,1)} %param.6, s32[1600]{0:T(1024)S(1)} %xor.34), kind=kOutput, calls=%fused_computation.2 | convolution fusion | flops 10262400000 | bytes 26524960 | tf_op jit(solution)/shard_map/dot_general | solution.py:56
  150.9 2.6 pad_maximum_fusion
  153.5 107.4 %all-reduce.1 = bf16[768,1600]{1,0:T(8,128)(2,1)S(1)} all-reduce(f32[768,1600]{1,0:T(8,128)} %pad_maximum_fusion), channel_id=1, replica_groups=mesh['row'=8,'col'=16] {'row','col'}, use_global_device_ids=true, to_apply=%region_12.13 | all-reduce | flops 1228800 | bytes 7372800 | tf_op jit(solution)/shard_map/psum | solution.py:64
  260.9 0.1 dynamic-slice_convert_fusion
  261.0 0.1 concatenate.8
  261.1 0.7 broadcast_select_fusion
  (14 shorter events, 0.1 us)
Async XLA Ops:
  7.3 34.7 %all-to-all-start = ((bf16[16,8,5000]{2,1,0:T(8,128)(2,1)}), bf16[16,8,5000]{2,1,0:T(8,128)(2,1)S(1)}, u32[]{:S(2)}, u32[]{:S(2)}) async-start(bf16[16,8,5000]{2,1,0:T(8,128)(2,1)} %bitcast.17), calls=%async_computation | async-start | bytes 2621440 | tf_op jit(solution)/shard_map/all_to_all | solution.py:45
  42.1 7.5 %copy-start = (s32[384]{0:T(512)S(1)}, s32[384]{0:T(512)}, u32[]{:S(2)}) copy-start(s32[384]{0:T(512)} %param.9) | copy-start | bytes 4612
  42.1 17.4 %copy-start.1 = (s32[800]{0:T(1024)S(1)}, s32[800]{0:T(1024)}, u32[]{:S(2)}) copy-start(s32[800]{0:T(1024)} %param.8) | copy-start | bytes 9604
  42.1 17.8 %copy-start.2 = (s32[120]{0:T(128)S(1)}, s32[120]{0:T(128)}, u32[]{:S(2)}) copy-start(s32[120]{0:T(128)} %param.7) | copy-start | bytes 1444
  42.1 84.5 %all-to-all-start.1 = ((bf16[16,40,5000]{2,1,0:T(8,128)(2,1)}), bf16[16,40,5000]{2,1,0:T(8,128)(2,1)}, u32[]{:S(2)}, u32[]{:S(2)}) async-start(bf16[16,40,5000]{2,1,0:T(8,128)(2,1)} %bitcast.18), calls=%async_computation.1 | async-start | bytes 13107200 | tf_op jit(solution)/shard_map/all_to_all | solution.py:45

commit v9 on v4

--- a/solution.py
+++ b/solution.py
@@ -36,9 +36,13 @@
     masked_v = jnp.where(cd_irrep[:, None] == ab_irrep[None, :], integrals, zero_half)
     rows_piece = local_pairs // PIECES
     terms = []
+    source_rows = amplitudes
     for h in range(PIECES):
-        part = amplitudes[h * rows_piece:(h + 1) * rows_piece]
-        panel = lax.all_to_all(part, "col", split_axis=1, concat_axis=0, tiled=True)
+        rows_h = source_rows[h * rows_piece:(h + 1) * rows_piece]
+        part = jnp.transpose(rows_h.reshape(rows_piece, ncols, cd_dev), (1, 0, 2))
+        source_rows, part = lax.optimization_barrier((source_rows, part))
+        panel = lax.all_to_all(part, "col", split_axis=0, concat_axis=0, tiled=True)
+        panel = panel.reshape(ncols * rows_piece, cd_dev)
         piece_pairs = (
             jnp.arange(ncols, dtype=jnp.int32)[:, None] * local_pairs
             + h * rows_piece
@@ -49,14 +53,13 @@
         )
         masked_t = jnp.where(piece_irrep[:, None] == cd_irrep[None, :], panel, zero_half)
         terms.append(jnp.dot(masked_t, masked_v, preferred_element_type=jnp.float32))
-    total = jnp.concatenate(terms, axis=0)
     ntiles = tile_owner.shape[0]
     tile_ids = jnp.arange(ntiles, dtype=jnp.int32)
     same = tile_owner[:, None] == tile_owner[None, :]
     earlier = tile_ids[:, None] > tile_ids[None, :]
     rank = jnp.sum(jnp.where(same & earlier, 1, 0), axis=1).astype(jnp.int32)
     slot = tile_owner * CAP + rank
-    summed = lax.psum(total, ("row", "col"))
+    summed = lax.psum(tuple(terms), ("row", "col"))
     wanted = myself * CAP + jnp.arange(CAP, dtype=jnp.int32)
     match = slot[None, :] == wanted[:, None]
     source = jnp.sum(jnp.where(match, tile_ids[None, :], 0), axis=1)
@@ -67,9 +70,16 @@
     which = (within // rows_piece).reshape(CAP * TR)
     rows = (sender * rows_piece + within % rows_piece).reshape(CAP * TR)
     keep = jnp.repeat(found, TR)
-    flat_rows = which * (ncols * rows_piece) + rows
-    summed = summed.reshape(PIECES * ncols * rows_piece, ab_width)
-    picked = jnp.take(summed, flat_rows, axis=0).astype(jnp.bfloat16)
+    which = which.reshape(CAP, TR)[:, 0]
+    starts = rows.reshape(CAP, TR)[:, 0]
+    pieces = []
+    for k in range(CAP):
+        options = [lax.dynamic_slice_in_dim(s, starts[k], TR, axis=0) for s in summed]
+        chosen = options[0]
+        for h in range(1, PIECES):
+            chosen = jnp.where(which[k] == h, options[h], chosen)
+        pieces.append(chosen)
+    picked = jnp.concatenate(pieces, axis=0).astype(jnp.bfloat16)
     placed = jnp.where(keep[:, None], picked, zero_half)
     return placed.reshape(CAP * TR, ab_width)
 

time: 261 us -> 262 us (level)
  waiting for transfers between devices: 66.4 us -> 45.8 us
  between operations: 0.19 us -> 15.4 us
  matrix products: 26.6 us -> 29.3 us
    all_to_all x4 -> x0, local copies, waits for them, and re-layouts: 29.3 us -> none  [on_device(): panel = lax.all_to_all(part, 'col', split_axis=1, concat_axis=0, tiled=True)]
    reshape x0 -> x4, local copies, waits for them, and re-layouts: none -> 29.3 us  [on_device(): part = jnp.transpose(rows_h.reshape(rows_piece, ncols, cd_dev), (1, 0, 2))]
    all_to_all x2, waiting for transfers between devices: 66.4 us -> 45.8 us  [on_device(): panel = lax.all_to_all(part, 'col', split_axis=0, concat_axis=0, tiled=True)]
    select_n x0 -> x6, local copies, waits for them, and re-layouts: none -> 5.24 us  [on_device(): chosen = jnp.where(which[k] == h, options[h], chosen)]
    psum x1 -> x0, local copies, waits for them, and re-layouts: 3.98 us -> none  [on_device(): summed = lax.psum(total, ('row', 'col'))]
    slice x1 -> x3, local copies, waits for them, and re-layouts: 5.55 us -> 9.06 us  [the longest x2 8.43 us: on_device(): rows_h = source_rows[h * rows_piece:(h + 1) * rows_piece]]
    select_n x1 -> x2, other arithmetic: 0.02 us -> 3.14 us  [the longest x1 3.05 us: on_device(): chosen = jnp.where(which[k] == h, options[h], chosen)]
    dot_general x2, matrix products: 26.6 us -> 29.3 us  [on_device(): jnp.dot(masked_t, masked_v, preferred_element_type=jnp.float32)]
  transfers between devices with their start and end apart: 2 -> 2, of which waited for: 2 -> 2; matrix products, arithmetic and copies ran while one was open for 9% -> 14% of each run, Pallas kernels for 0% -> 0%
where the time goes in v9:
time: 262 us; the launch traced here: 261 us
  blocking collectives  109 us (42%)
  waiting for transfers between devices  45.8 us (17%)
  local copies, waits for them, and re-layouts  44.4 us (17%)
  matrix products  29.3 us (11%)
  between operations  15.4 us (6%)
  starting transfers between devices  12 us (5%)
  other arithmetic  5.62 us (2%)
    psum x1, blocking collectives, on_device(): summed = lax.psum(tuple(terms), ('row', 'col'))  109 us
    all_to_all x2, waiting for transfers between devices, on_device(): panel = lax.all_to_all(part, 'col', split_axis=0, concat_axis=0, tiled=True)  45.8 us
    dot_general x2, matrix products, on_device(): jnp.dot(masked_t, masked_v, preferred_element_type=jnp.float32)  29.3 us
    reshape x4, local copies, waits for them, and re-layouts, on_device(): part = jnp.transpose(rows_h.reshape(rows_piece, ncols, cd_dev), (1, 0, 2))  29.3 us
    all_to_all x2, starting transfers between devices, on_device(): panel = lax.all_to_all(part, 'col', split_axis=0, concat_axis=0, tiled=True)  12 us
    slice x2, local copies, waits for them, and re-layouts, on_device(): rows_h = source_rows[h * rows_piece:(h + 1) * rows_piece]  8.43 us
    select_n x6, local copies, waits for them, and re-layouts, on_device(): chosen = jnp.where(which[k] == h, options[h], chosen)  5.24 us
  transfers between devices with their start and end apart: 2, of which 2 were waited for; matrix products, arithmetic and copies ran while one was open for 14% of the time, Pallas kernels for 0%

profile of v9, /device:TPU:0, one launch (start us, length us, event | category | flops | bytes accessed | tf_op | source)
XLA Modules:
  0.0 261.2 jit_solution(5659829424453791409)
XLA Ops:
  0.0 4.2 %slice.75 = bf16[24,80000]{1,0:T(8,128)(2,1)} slice(bf16[48,80000]{1,0:T(8,128)(2,1)} %param.5), slice={[0:24], [0:80000]} | slice | bytes 7680000 | tf_op jit(solution)/shard_map/slice | solution.py:41
  4.2 8.4 %reshape.214 = bf16[24,16,5000]{2,1,0:T(8,128)(2,1)} reshape(bf16[24,80000]{1,0:T(8,128)(2,1)} %slice.75) | data formatting | bytes 7680000 | tf_op jit(solution)/shard_map/reshape | solution.py:42
  12.7 6.3 %copy.29 = bf16[24,16,5000]{2,0,1:T(8,128)(2,1)} copy(bf16[24,16,5000]{2,1,0:T(8,128)(2,1)} %reshape.214) | data formatting | bytes 7680000 | tf_op jit(solution)/shard_map/reshape | solution.py:42
  18.9 0.0 copy-start
  18.9 7.3 %all-to-all-start.1 = ((bf16[16,24,5000]{2,1,0:T(8,128)(2,1)}), bf16[16,24,5000]{2,1,0:T(8,128)(2,1)}, u32[]{:S(2)}, u32[]{:S(2)}) async-start(bf16[16,24,5000]{2,1,0:T(8,128)(2,1)} %bitcast.21), calls=%async_computation.1 | async-start | bytes 7864320 | tf_op jit(solution)/shard_map/all_to_all | solution.py:44
  26.3 0.0 copy-done
  26.3 0.2 select_reduce_fusion
  26.5 0.2 fusion.18
  26.7 0.1 add_select_fusion.5
  26.8 0.6 fusion.40
  35.0 0.1 fusion.23
  35.1 0.1 rem.121
  35.2 0.1 div.61
  35.2 0.1 sign_compare_fusion.1
  35.3 0.1 ne.196
  35.4 0.1 fusion.24
  35.5 0.1 rem.114
  35.6 0.1 div.56
  35.7 4.2 %slice.76 = bf16[24,80000]{1,0:T(8,128)(2,1)} slice(bf16[48,80000]{1,0:T(8,128)(2,1)} %param.5), slice={[24:48], [0:80000]} | slice | bytes 7680000 | tf_op jit(solution)/shard_map/slice | solution.py:41
  39.9 8.4 %reshape.215 = bf16[24,16,5000]{2,1,0:T(8,128)(2,1)} reshape(bf16[24,80000]{1,0:T(8,128)(2,1)} %slice.76) | data formatting | bytes 7680000 | tf_op jit(solution)/shard_map/reshape | solution.py:42
  48.3 6.2 %copy.28 = bf16[24,16,5000]{2,0,1:T(8,128)(2,1)} copy(bf16[24,16,5000]{2,1,0:T(8,128)(2,1)} %reshape.215) | data formatting | bytes 7680000 | tf_op jit(solution)/shard_map/reshape | solution.py:42
  54.5 20.7 %all-to-all-done.1 = bf16[16,24,5000]{2,1,0:T(8,128)(2,1)} async-done(((bf16[16,24,5000]{2,1,0:T(8,128)(2,1)}), bf16[16,24,5000]{2,1,0:T(8,128)(2,1)}, u32[]{:S(2)}, u32[]{:S(2)}) %all-to-all-start.1) | async-done | bytes 3840032 | tf_op jit(solution)/shard_map/all_to_all | solution.py:44
  75.2 4.7 %all-to-all-start = ((bf16[16,24,5000]{2,1,0:T(8,128)(2,1)}), bf16[16,24,5000]{2,1,0:T(8,128)(2,1)}, u32[]{:S(2)}, u32[]{:S(2)}) async-start(bf16[16,24,5000]{2,1,0:T(8,128)(2,1)} %bitcast.20), calls=%async_computation | async-start | bytes 7864320 | tf_op jit(solution)/shard_map/all_to_all | solution.py:44
  79.9 0.1 sign_compare_fusion.2
  80.0 0.1 ne.183
  84.0 0.2 compare_reduce_fusion
  84.2 0.1 broadcast_in_dim.37
  84.3 0.1 broadcast_in_dim.38
  84.4 0.0 copy-done.1
  84.4 0.2 convert_reduce_fusion.4
  84.6 0.2 convert_reduce_fusion
  84.8 0.1 convert_reduce_fusion.2
  84.9 0.0 copy-done.2
  84.9 0.2 convert_reduce_fusion.9
  85.1 0.1 convert_reduce_fusion.7
  89.0 14.7 %fusion = f32[384,1600]{0,1:T(8,128)} fusion(bf16[5000,1600]{0,1:T(8,128)(2,1)} %param.6, s32[5000]{0:T(1024)S(1)} %xor.33, s32[1600]{0:T(1024)S(1)} %xor.34, bf16[384,5000]{1,0:T(8,128)(2,1)} %bitcast.5, s32[384]{0:T(512)S(1)} %xor.35), kind=kOutput, calls=%fused_computation.3 | convolution fusion | flops 6163840000 | bytes 22325536 | tf_op jit(solution)/shard_map/dot_general | solution.py:55
  103.7 25.0 %all-to-all-done = bf16[16,24,5000]{2,1,0:T(8,128)(2,1)} async-done(((bf16[16,24,5000]{2,1,0:T(8,128)(2,1)}), bf16[16,24,5000]{2,1,0:T(8,128)(2,1)}, u32[]{:S(2)}, u32[]{:S(2)}) %all-to-all-start) | async-done | bytes 3840032 | tf_op jit(solution)/shard_map/all_to_all | solution.py:44
  128.7 14.6 %fusion.1 = f32[384,1600]{0,1:T(8,128)} fusion(bf16[5000,1600]{0,1:T(8,128)(2,1)} %param.6, s32[5000]{0:T(1024)S(1)} %xor.33, s32[1600]{0:T(1024)S(1)} %xor.34, bf16[384,5000]{1,0:T(8,128)(2,1)} %bitcast.3, s32[384]{0:T(512)S(1)} %xor.32), kind=kOutput, calls=%fused_computation.4 | convolution fusion | flops 6163840000 | bytes 22325536 | tf_op jit(solution)/shard_map/dot_general | solution.py:55
  143.3 108.7 %all-reduce.2 = (bf16[384,1600]{0,1:T(8,128)(2,1)S(1)}, bf16[384,1600]{0,1:T(8,128)(2,1)S(1)}) all-reduce(f32[384,1600]{0,1:T(8,128)} %fusion, f32[384,1600]{0,1:T(8,128)} %fusion.1), channel_id=1, replica_groups=mesh['row'=8,'col'=16] {'row','col'}, use_global_device_ids=true, to_apply=%region_14.15 | all-reduce | flops 1228800 | bytes 7372800 | tf_op jit(solution)/shard_map/psum | solution.py:62
  252.1 3.0 %dynamic-slice_select_fusion = (bf16[2,1600]{0,1:T(8,128)(2,1)S(1)}, bf16[2,1600]{0,1:T(8,128)(2,1)S(1)}, bf16[2,1600]{0,1:T(8,128)(2,1)}, bf16[2,1600]{0,1:T(8,...) fusion(bf16[384,1600]{0,1:T(8,128)(2,1)S(1)} %get-tuple-element.19, s32[]{:T(128)S(6)} %select_n.209, ...), kind=kLoop, calls=%fused_computation.13 | loop fusion | flops 19200 | bytes 115230 | tf_op jit(solution)/shard_map/jit(_where)/select_n | solution.py:80
  255.1 1.2 copy.20
  256.3 1.2 copy.21
  257.5 1.2 copy.22
  258.7 1.2 copy.23
  260.0 0.2 copy.24
  260.2 0.2 copy.25
  260.4 0.1 concatenate.4
  260.5 0.7 broadcast_select_fusion
  (15 shorter events, 0.1 us)
Async XLA Ops:
  18.9 7.4 %copy-start = (s32[384]{0:T(512)S(1)}, s32[384]{0:T(512)}, u32[]{:S(2)}) copy-start(s32[384]{0:T(512)} %param.9) | copy-start | bytes 4612
  18.9 56.3 %all-to-all-start.1 = ((bf16[16,24,5000]{2,1,0:T(8,128)(2,1)}), bf16[16,24,5000]{2,1,0:T(8,128)(2,1)}, u32[]{:S(2)}, u32[]{:S(2)}) async-start(bf16[16,24,5000]{2,1,0:T(8,128)(2,1)} %bitcast.21), calls=%async_computation.1 | async-start | bytes 7864320 | tf_op jit(solution)/shard_map/all_to_all | solution.py:44
  54.5 29.9 %copy-start.1 = (s32[800]{0:T(1024)S(1)}, s32[800]{0:T(1024)}, u32[]{:S(2)}) copy-start(s32[800]{0:T(1024)} %param.8) | copy-start | bytes 9604
  54.5 30.4 %copy-start.2 = (s32[120]{0:T(128)S(1)}, s32[120]{0:T(128)}, u32[]{:S(2)}) copy-start(s32[120]{0:T(128)} %param.7) | copy-start | bytes 1444
  75.2 53.5 %all-to-all-start = ((bf16[16,24,5000]{2,1,0:T(8,128)(2,1)}), bf16[16,24,5000]{2,1,0:T(8,128)(2,1)}, u32[]{:S(2)}, u32[]{:S(2)}) async-start(bf16[16,24,5000]{2,1,0:T(8,128)(2,1)} %bitcast.20), calls=%async_computation | async-start | bytes 7864320 | tf_op jit(solution)/shard_map/all_to_all | solution.py:44

commit v10 on v9

--- a/solution.py
+++ b/solution.py
@@ -70,16 +70,15 @@
     which = (within // rows_piece).reshape(CAP * TR)
     rows = (sender * rows_piece + within % rows_piece).reshape(CAP * TR)
     keep = jnp.repeat(found, TR)
-    which = which.reshape(CAP, TR)[:, 0]
-    starts = rows.reshape(CAP, TR)[:, 0]
-    pieces = []
-    for k in range(CAP):
-        options = [lax.dynamic_slice_in_dim(s, starts[k], TR, axis=0) for s in summed]
-        chosen = options[0]
-        for h in range(1, PIECES):
-            chosen = jnp.where(which[k] == h, options[h], chosen)
-        pieces.append(chosen)
-    picked = jnp.concatenate(pieces, axis=0).astype(jnp.bfloat16)
+    picked = None
+    for h in range(PIECES):
+        hits = (which == h)[:, None] & (
+            rows[:, None] == jnp.arange(summed[h].shape[0], dtype=jnp.int32)[None, :]
+        )
+        picker = hits.astype(summed[h].dtype)
+        term = jnp.dot(picker, summed[h], preferred_element_type=jnp.float32)
+        picked = term if picked is None else picked + term
+    picked = picked.astype(jnp.bfloat16)
     placed = jnp.where(keep[:, None], picked, zero_half)
     return placed.reshape(CAP * TR, ab_width)
 

time: 262 us -> 257 us (0.981)
  waiting for transfers between devices: 45.8 us -> 62.4 us
  between operations: 15.4 us -> 0.19 us
  local copies, waits for them, and re-layouts: 44.4 us -> 38.8 us
  other arithmetic: 5.62 us -> 1.97 us
  matrix products: 29.3 us -> 32 us
    all_to_all x2, waiting for transfers between devices: 45.8 us -> 62.4 us  [on_device(): panel = lax.all_to_all(part, 'col', split_axis=0, concat_axis=0, tiled=True)]
    select_n x6 -> x0, local copies, waits for them, and re-layouts: 5.24 us -> none  [on_device(): chosen = jnp.where(which[k] == h, options[h], chosen)]
    dot_general x0 -> x2, matrix products: none -> 4.09 us  [on_device(): term = jnp.dot(picker, summed[h], preferred_element_type=jnp.float32)]
    select_n x4 -> x1, other arithmetic: 3.85 us -> 0.01 us  [on_device(): piece_pairs // norb]
where the time goes in v10:
time: 257 us; the launch traced here: 256 us
  blocking collectives  109 us (42%)
  waiting for transfers between devices  62.4 us (24%)
  local copies, waits for them, and re-layouts  38.8 us (15%)
  matrix products  32 us (12%)
  starting transfers between devices  11.9 us (5%)
    psum x1, blocking collectives, on_device(): summed = lax.psum(tuple(terms), ('row', 'col'))  109 us
    all_to_all x2, waiting for transfers between devices, on_device(): panel = lax.all_to_all(part, 'col', split_axis=0, concat_axis=0, tiled=True)  62.4 us
    reshape x4, local copies, waits for them, and re-layouts, on_device(): part = jnp.transpose(rows_h.reshape(rows_piece, ncols, cd_dev), (1, 0, 2))  29.3 us
    dot_general x2, matrix products, on_device(): jnp.dot(masked_t, masked_v, preferred_element_type=jnp.float32)  28 us
    all_to_all x2, starting transfers between devices, on_device(): panel = lax.all_to_all(part, 'col', split_axis=0, concat_axis=0, tiled=True)  11.9 us
    slice x2, local copies, waits for them, and re-layouts, on_device(): rows_h = source_rows[h * rows_piece:(h + 1) * rows_piece]  8.52 us
  transfers between devices with their start and end apart: 2, of which 2 were waited for; matrix products, arithmetic and copies ran while one was open for 14% of the time, Pallas kernels for 0%

profile of v10, /device:TPU:0, one launch (start us, length us, event | category | flops | bytes accessed | tf_op | source)
XLA Modules:
  0.0 256.1 jit_solution(10140193772043384206)
XLA Ops:
  0.0 4.2 %slice.6 = bf16[24,80000]{1,0:T(8,128)(2,1)} slice(bf16[48,80000]{1,0:T(8,128)(2,1)} %param.5), slice={[0:24], [0:80000]} | slice | bytes 7680000 | tf_op jit(solution)/shard_map/slice | solution.py:41
  4.2 8.4 %reshape.242 = bf16[24,16,5000]{2,1,0:T(8,128)(2,1)} reshape(bf16[24,80000]{1,0:T(8,128)(2,1)} %slice.6) | data formatting | bytes 7680000 | tf_op jit(solution)/shard_map/reshape | solution.py:42
  12.7 6.2 %copy.13 = bf16[24,16,5000]{2,0,1:T(8,128)(2,1)} copy(bf16[24,16,5000]{2,1,0:T(8,128)(2,1)} %reshape.242) | data formatting | bytes 7680000 | tf_op jit(solution)/shard_map/reshape | solution.py:42
  18.8 7.2 %all-to-all-start = ((bf16[16,24,5000]{2,1,0:T(8,128)(2,1)}), bf16[16,24,5000]{2,1,0:T(8,128)(2,1)}, u32[]{:S(2)}, u32[]{:S(2)}) async-start(bf16[16,24,5000]{2,1,0:T(8,128)(2,1)} %bitcast.11), calls=%async_computation | async-start | bytes 7864320 | tf_op jit(solution)/shard_map/all_to_all | solution.py:44
  26.0 0.1 sign_compare_fusion.2
  26.1 0.1 ne.241
  26.2 0.1 sign_compare_fusion.1
  26.3 0.1 ne.253
  26.4 0.1 fusion.33
  26.5 0.1 div.77
  26.6 0.1 rem.151
  26.7 0.1 fusion.35
  26.7 0.1 div.73
  26.8 0.1 rem.144
  26.9 4.3 %slice.7 = bf16[24,80000]{1,0:T(8,128)(2,1)} slice(bf16[48,80000]{1,0:T(8,128)(2,1)} %param.5), slice={[24:48], [0:80000]} | slice | bytes 7680000 | tf_op jit(solution)/shard_map/slice | solution.py:41
  31.2 8.4 %reshape.244 = bf16[24,16,5000]{2,1,0:T(8,128)(2,1)} reshape(bf16[24,80000]{1,0:T(8,128)(2,1)} %slice.7) | data formatting | bytes 7680000 | tf_op jit(solution)/shard_map/reshape | solution.py:42
  39.6 0.0 copy-start
  39.6 6.3 %copy.12 = bf16[24,16,5000]{2,0,1:T(8,128)(2,1)} copy(bf16[24,16,5000]{2,1,0:T(8,128)(2,1)} %reshape.244) | data formatting | bytes 7680000 | tf_op jit(solution)/shard_map/reshape | solution.py:42
  45.9 0.0 copy-done
  45.9 0.2 select_reduce_fusion
  46.2 0.2 fusion.25
  46.3 0.2 compare_reduce_fusion
  46.5 0.1 sign_compare_fusion.3
  46.6 0.1 fusion.38
  46.7 0.0 copy-start.2
  46.7 0.0 copy-start.1
  46.7 28.3 %all-to-all-done = bf16[16,24,5000]{2,1,0:T(8,128)(2,1)} async-done(((bf16[16,24,5000]{2,1,0:T(8,128)(2,1)}), bf16[16,24,5000]{2,1,0:T(8,128)(2,1)}, u32[]{:S(2)}, u32[]{:S(2)}) %all-to-all-start) | async-done | bytes 3840032 | tf_op jit(solution)/shard_map/all_to_all | solution.py:44
  75.0 4.7 %all-to-all-start.1 = ((bf16[16,24,5000]{2,1,0:T(8,128)(2,1)}), bf16[16,24,5000]{2,1,0:T(8,128)(2,1)}, u32[]{:S(2)}, u32[]{:S(2)}) async-start(bf16[16,24,5000]{2,1,0:T(8,128)(2,1)} %bitcast.10), calls=%async_computation.1 | async-start | bytes 7864320 | tf_op jit(solution)/shard_map/all_to_all | solution.py:44
  79.7 0.0 copy-done.2
  79.7 0.2 convert_reduce_fusion.9
  79.9 0.1 broadcast_in_dim.37
  80.0 0.1 broadcast_in_dim.38
  80.1 0.1 ne.238
  80.2 0.1 rem.138
  80.3 0.1 div.71
  80.3 0.1 convert_reduce_fusion.5
  80.5 0.0 copy-done.1
  80.5 0.2 convert_reduce_fusion.4
  80.7 0.1 convert_reduce_fusion.2
  80.8 0.2 convert_reduce_fusion
  81.1 13.3 %fusion.1 = f32[384,1600]{0,1:T(8,128)S(1)} fusion(bf16[5000,1600]{0,1:T(8,128)(2,1)} %param.6, s32[5000]{0:T(1024)S(1)} %xor.33, s32[1600]{0:T(1024)S(1)} %xor.34, bf16[384,5000]{1,0:T(8,128)(2,1)} %bitcast.1, s32[384]{0:T(512)S(1)} %xor.32), kind=kOutput, calls=%fused_computation.4 | convolution fusion | flops 6163840000 | bytes 22325536 | tf_op jit(solution)/shard_map/dot_general | solution.py:55
  94.4 34.1 %all-to-all-done.1 = bf16[16,24,5000]{2,1,0:T(8,128)(2,1)} async-done(((bf16[16,24,5000]{2,1,0:T(8,128)(2,1)}), bf16[16,24,5000]{2,1,0:T(8,128)(2,1)}, u32[]{:S(2)}, u32[]{:S(2)}) %all-to-all-start.1) | async-done | bytes 3840032 | tf_op jit(solution)/shard_map/all_to_all | solution.py:44
  128.5 14.6 %fusion = f32[384,1600]{0,1:T(8,128)} fusion(bf16[5000,1600]{0,1:T(8,128)(2,1)} %param.6, s32[5000]{0:T(1024)S(1)} %xor.33, s32[1600]{0:T(1024)S(1)} %xor.34, bf16[384,5000]{1,0:T(8,128)(2,1)} %bitcast.3, s32[384]{0:T(512)S(1)} %xor.35), kind=kOutput, calls=%fused_computation.3 | convolution fusion | flops 6163840000 | bytes 22325536 | tf_op jit(solution)/shard_map/dot_general | solution.py:55
  143.1 108.9 %all-reduce.2 = (bf16[384,1600]{0,1:T(8,128)(2,1)}, bf16[384,1600]{0,1:T(8,128)(2,1)}) all-reduce(f32[384,1600]{0,1:T(8,128)S(1)} %fusion.1, f32[384,1600]{0,1:T(8,128)} %fusion), channel_id=1, replica_groups=mesh['row'=8,'col'=16] {'row','col'}, use_global_device_ids=true, to_apply=%region_11.12 | all-reduce | flops 1228800 | bytes 7372800 | tf_op jit(solution)/shard_map/psum | solution.py:62
  252.0 1.7 fusion.13
  253.7 2.4 fusion.7
  (16 shorter events, 0.1 us)
Async XLA Ops:
  18.8 56.2 %all-to-all-start = ((bf16[16,24,5000]{2,1,0:T(8,128)(2,1)}), bf16[16,24,5000]{2,1,0:T(8,128)(2,1)}, u32[]{:S(2)}, u32[]{:S(2)}) async-start(bf16[16,24,5000]{2,1,0:T(8,128)(2,1)} %bitcast.11), calls=%async_computation | async-start | bytes 7864320 | tf_op jit(solution)/shard_map/all_to_all | solution.py:44
  39.6 6.3 %copy-start = (s32[384]{0:T(512)S(1)}, s32[384]{0:T(512)}, u32[]{:S(2)}) copy-start(s32[384]{0:T(512)} %param.9) | copy-start | bytes 4612
  46.7 33.0 %copy-start.2 = (s32[120]{0:T(128)S(1)}, s32[120]{0:T(128)}, u32[]{:S(2)}) copy-start(s32[120]{0:T(128)} %param.7) | copy-start | bytes 1444
  46.7 33.8 %copy-start.1 = (s32[800]{0:T(1024)S(1)}, s32[800]{0:T(1024)}, u32[]{:S(2)}) copy-start(s32[800]{0:T(1024)} %param.8) | copy-start | bytes 9604
  75.0 53.5 %all-to-all-start.1 = ((bf16[16,24,5000]{2,1,0:T(8,128)(2,1)}), bf16[16,24,5000]{2,1,0:T(8,128)(2,1)}, u32[]{:S(2)}, u32[]{:S(2)}) async-start(bf16[16,24,5000]{2,1,0:T(8,128)(2,1)} %bitcast.10), calls=%async_computation.1 | async-start | bytes 7864320 | tf_op jit(solution)/shard_map/all_to_all | solution.py:44

commit v11 on v10

--- a/solution.py
+++ b/solution.py
@@ -34,6 +34,7 @@
         lookup(vir_irrep, cd_index // nvirt), lookup(vir_irrep, cd_index % nvirt)
     )
     masked_v = jnp.where(cd_irrep[:, None] == ab_irrep[None, :], integrals, zero_half)
+    masked_v = lax.optimization_barrier(masked_v)
     rows_piece = local_pairs // PIECES
     terms = []
     source_rows = amplitudes

time: 257 us -> 257 us (level)
  other arithmetic: 1.97 us -> 16.8 us
  waiting for transfers between devices: 62.4 us -> 47.7 us
    select_n x0 -> x1, other arithmetic: none -> 14.9 us  [on_device(): jnp.where(cd_irrep[:, None] == ab_irrep[None, :], integrals, zero_half)]
    all_to_all x2, waiting for transfers between devices: 62.4 us -> 47.7 us  [on_device(): panel = lax.all_to_all(part, 'col', split_axis=0, concat_axis=0, tiled=True)]
  transfers between devices with their start and end apart: 2 -> 2, of which waited for: 2 -> 2; matrix products, arithmetic and copies ran while one was open for 14% -> 19% of each run, Pallas kernels for 0% -> 0%
where the time goes in v11:
time: 257 us; the launch traced here: 256 us
  blocking collectives  109 us (42%)
  waiting for transfers between devices  47.7 us (19%)
  local copies, waits for them, and re-layouts  38.7 us (15%)
  matrix products  31.8 us (12%)
  other arithmetic  16.8 us (7%)
  starting transfers between devices  12 us (5%)
    psum x1, blocking collectives, on_device(): summed = lax.psum(tuple(terms), ('row', 'col'))  109 us
    all_to_all x2, waiting for transfers between devices, on_device(): panel = lax.all_to_all(part, 'col', split_axis=0, concat_axis=0, tiled=True)  47.7 us
    reshape x4, local copies, waits for them, and re-layouts, on_device(): part = jnp.transpose(rows_h.reshape(rows_piece, ncols, cd_dev), (1, 0, 2))  29.3 us
    dot_general x2, matrix products, on_device(): jnp.dot(masked_t, masked_v, preferred_element_type=jnp.float32)  27.7 us
    select_n x1, other arithmetic, on_device(): jnp.where(cd_irrep[:, None] == ab_irrep[None, :], integrals, zero_half)  14.9 us
    all_to_all x2, starting transfers between devices, on_device(): panel = lax.all_to_all(part, 'col', split_axis=0, concat_axis=0, tiled=True)  12 us
    slice x2, local copies, waits for them, and re-layouts, on_device(): rows_h = source_rows[h * rows_piece:(h + 1) * rows_piece]  8.43 us
  transfers between devices with their start and end apart: 2, of which 2 were waited for; matrix products, arithmetic and copies ran while one was open for 19% of the time, Pallas kernels for 0%

profile of v11, /device:TPU:0, one launch (start us, length us, event | category | flops | bytes accessed | tf_op | source)
XLA Modules:
  0.0 256.1 jit_solution(16155034870048202088)
XLA Ops:
  0.0 4.2 %slice.6 = bf16[24,80000]{1,0:T(8,128)(2,1)} slice(bf16[48,80000]{1,0:T(8,128)(2,1)} %param.5), slice={[0:24], [0:80000]} | slice | bytes 7680000 | tf_op jit(solution)/shard_map/slice | solution.py:42
  4.2 8.4 %reshape.242 = bf16[24,16,5000]{2,1,0:T(8,128)(2,1)} reshape(bf16[24,80000]{1,0:T(8,128)(2,1)} %slice.6) | data formatting | bytes 7680000 | tf_op jit(solution)/shard_map/reshape | solution.py:43
  12.7 6.2 %copy.13 = bf16[24,16,5000]{2,0,1:T(8,128)(2,1)} copy(bf16[24,16,5000]{2,1,0:T(8,128)(2,1)} %reshape.242) | data formatting | bytes 7680000 | tf_op jit(solution)/shard_map/reshape | solution.py:43
  18.8 0.0 copy-start
  18.8 7.3 %all-to-all-start = ((bf16[16,24,5000]{2,1,0:T(8,128)(2,1)}), bf16[16,24,5000]{2,1,0:T(8,128)(2,1)}, u32[]{:S(2)}, u32[]{:S(2)}) async-start(bf16[16,24,5000]{2,1,0:T(8,128)(2,1)} %bitcast.13), calls=%async_computation | async-start | bytes 7864320 | tf_op jit(solution)/shard_map/all_to_all | solution.py:45
  26.2 0.1 sign_compare_fusion.2
  26.3 0.0 copy-done
  26.3 0.2 select_reduce_fusion
  26.5 0.2 fusion.25
  26.7 0.1 sign_compare_fusion.3
  26.8 4.2 %slice.7 = bf16[24,80000]{1,0:T(8,128)(2,1)} slice(bf16[48,80000]{1,0:T(8,128)(2,1)} %param.5), slice={[24:48], [0:80000]} | slice | bytes 7680000 | tf_op jit(solution)/shard_map/slice | solution.py:42
  31.1 8.4 %reshape.244 = bf16[24,16,5000]{2,1,0:T(8,128)(2,1)} reshape(bf16[24,80000]{1,0:T(8,128)(2,1)} %slice.7) | data formatting | bytes 7680000 | tf_op jit(solution)/shard_map/reshape | solution.py:43
  39.5 0.0 copy-start.1
  39.5 6.3 %copy.12 = bf16[24,16,5000]{2,0,1:T(8,128)(2,1)} copy(bf16[24,16,5000]{2,1,0:T(8,128)(2,1)} %reshape.244) | data formatting | bytes 7680000 | tf_op jit(solution)/shard_map/reshape | solution.py:43
  45.8 0.0 copy-done.1
  45.8 0.2 convert_reduce_fusion.4
  46.0 0.1 convert_reduce_fusion.2
  46.1 0.2 convert_reduce_fusion
  46.3 0.1 sign_compare_fusion.1
  46.4 14.9 %compare_select_fusion = bf16[5000,1600]{0,1:T(8,128)(2,1)} fusion(bf16[5000,1600]{0,1:T(8,128)(2,1)} %param.6, s32[5000]{0:T(1024)S(1)} %xor.33, s32[1600]{0:T(1024)S(1)} %xor.34), kind=kLoop, calls=%fused_computation | loop fusion | flops 16000000 | bytes 32026400 | tf_op jit(solution)/shard_map/jit(_where)/select_n | solution.py:36
  61.2 0.0 copy-start.2
  61.2 13.9 %all-to-all-done = bf16[16,24,5000]{2,1,0:T(8,128)(2,1)} async-done(((bf16[16,24,5000]{2,1,0:T(8,128)(2,1)}), bf16[16,24,5000]{2,1,0:T(8,128)(2,1)}, u32[]{:S(2)}, u32[]{:S(2)}) %all-to-all-start) | async-done | bytes 3840032 | tf_op jit(solution)/shard_map/all_to_all | solution.py:45
  75.1 4.7 %all-to-all-start.1 = ((bf16[16,24,5000]{2,1,0:T(8,128)(2,1)}), bf16[16,24,5000]{2,1,0:T(8,128)(2,1)}, u32[]{:S(2)}, u32[]{:S(2)}) async-start(bf16[16,24,5000]{2,1,0:T(8,128)(2,1)} %bitcast.12), calls=%async_computation.1 | async-start | bytes 7864320 | tf_op jit(solution)/shard_map/all_to_all | solution.py:45
  79.8 0.2 compare_reduce_fusion
  80.0 0.1 ne.241
  80.1 0.1 ne.253
  80.2 0.1 broadcast_in_dim.37
  80.3 0.1 broadcast_in_dim.38
  80.4 0.1 ne.238
  80.5 0.1 fusion.38
  80.6 0.1 rem.138
  80.6 0.1 div.71
  80.7 0.1 fusion.33
  80.8 0.1 div.77
  80.9 0.1 rem.151
  81.0 0.1 fusion.35
  81.1 0.1 div.73
  81.2 0.1 rem.144
  81.3 0.0 copy-done.2
  81.3 0.2 convert_reduce_fusion.9
  81.5 0.1 convert_reduce_fusion.5
  81.6 13.2 %fusion = f32[384,1600]{0,1:T(8,128)S(1)} fusion(bf16[5000,1600]{0,1:T(8,128)(2,1)} %compare_select_fusion, bf16[384,5000]{1,0:T(8,128)(2,1)} %bitcast.1, s32[5000]{0:T(1024)S(1)} %xor.33, s32[384]{0:T(512)S(1)} %xor.32), kind=kOutput, calls=%fused_computation.3 | convolution fusion | flops 6147840000 | bytes 22319136 | tf_op jit(solution)/shard_map/dot_general | solution.py:56
  94.8 33.8 %all-to-all-done.1 = bf16[16,24,5000]{2,1,0:T(8,128)(2,1)} async-done(((bf16[16,24,5000]{2,1,0:T(8,128)(2,1)}), bf16[16,24,5000]{2,1,0:T(8,128)(2,1)}, u32[]{:S(2)}, u32[]{:S(2)}) %all-to-all-start.1) | async-done | bytes 3840032 | tf_op jit(solution)/shard_map/all_to_all | solution.py:45
  128.6 14.5 %fusion.1 = f32[384,1600]{0,1:T(8,128)} fusion(bf16[5000,1600]{0,1:T(8,128)(2,1)} %compare_select_fusion, bf16[384,5000]{1,0:T(8,128)(2,1)} %bitcast.3, s32[5000]{0:T(1024)S(1)} %xor.33, s32[384]{0:T(512)S(1)} %xor.35), kind=kOutput, calls=%fused_computation.4 | convolution fusion | flops 6147840000 | bytes 22319136 | tf_op jit(solution)/shard_map/dot_general | solution.py:56
  143.1 108.8 %all-reduce.2 = (bf16[384,1600]{0,1:T(8,128)(2,1)}, bf16[384,1600]{0,1:T(8,128)(2,1)}) all-reduce(f32[384,1600]{0,1:T(8,128)S(1)} %fusion, f32[384,1600]{0,1:T(8,128)} %fusion.1), channel_id=1, replica_groups=mesh['row'=8,'col'=16] {'row','col'}, use_global_device_ids=true, to_apply=%region_11.12 | all-reduce | flops 1228800 | bytes 7372800 | tf_op jit(solution)/shard_map/psum | solution.py:63
  252.0 1.7 fusion.13
  253.7 2.4 fusion.7
  (16 shorter events, 0.1 us)
Async XLA Ops:
  18.8 7.5 %copy-start = (s32[384]{0:T(512)S(1)}, s32[384]{0:T(512)}, u32[]{:S(2)}) copy-start(s32[384]{0:T(512)} %param.9) | copy-start | bytes 4612
  18.8 56.3 %all-to-all-start = ((bf16[16,24,5000]{2,1,0:T(8,128)(2,1)}), bf16[16,24,5000]{2,1,0:T(8,128)(2,1)}, u32[]{:S(2)}, u32[]{:S(2)}) async-start(bf16[16,24,5000]{2,1,0:T(8,128)(2,1)} %bitcast.13), calls=%async_computation | async-start | bytes 7864320 | tf_op jit(solution)/shard_map/all_to_all | solution.py:45
  39.5 6.3 %copy-start.1 = (s32[800]{0:T(1024)S(1)}, s32[800]{0:T(1024)}, u32[]{:S(2)}) copy-start(s32[800]{0:T(1024)} %param.8) | copy-start | bytes 9604
  61.2 20.0 %copy-start.2 = (s32[120]{0:T(128)S(1)}, s32[120]{0:T(128)}, u32[]{:S(2)}) copy-start(s32[120]{0:T(128)} %param.7) | copy-start | bytes 1444
  75.1 53.5 %all-to-all-start.1 = ((bf16[16,24,5000]{2,1,0:T(8,128)(2,1)}), bf16[16,24,5000]{2,1,0:T(8,128)(2,1)}, u32[]{:S(2)}, u32[]{:S(2)}) async-start(bf16[16,24,5000]{2,1,0:T(8,128)(2,1)} %bitcast.12), calls=%async_computation.1 | async-start | bytes 7864320 | tf_op jit(solution)/shard_map/all_to_all | solution.py:45

commit v12 on v10

--- a/solution.py
+++ b/solution.py
@@ -72,15 +72,14 @@
     keep = jnp.repeat(found, TR)
     picked = None
     for h in range(PIECES):
-        hits = (which == h)[:, None] & (
+        hits = ((which == h) & keep)[:, None] & (
             rows[:, None] == jnp.arange(summed[h].shape[0], dtype=jnp.int32)[None, :]
         )
         picker = hits.astype(summed[h].dtype)
         term = jnp.dot(picker, summed[h], preferred_element_type=jnp.float32)
         picked = term if picked is None else picked + term
     picked = picked.astype(jnp.bfloat16)
-    placed = jnp.where(keep[:, None], picked, zero_half)
-    return placed.reshape(CAP * TR, ab_width)
+    return picked.reshape(CAP * TR, ab_width)
 
 
 def solution(mesh):

time: 257 us -> 257 us (level)
  no operation moved by 1% of the time
where the time goes in v12:
time: 257 us; the launch traced here: 256 us
  blocking collectives  109 us (42%)
  waiting for transfers between devices  62.3 us (24%)
  local copies, waits for them, and re-layouts  38.8 us (15%)
  matrix products  32 us (12%)
  starting transfers between devices  11.9 us (5%)
    psum x1, blocking collectives, on_device(): summed = lax.psum(tuple(terms), ('row', 'col'))  109 us
    all_to_all x2, waiting for transfers between devices, on_device(): panel = lax.all_to_all(part, 'col', split_axis=0, concat_axis=0, tiled=True)  62.3 us
    reshape x4, local copies, waits for them, and re-layouts, on_device(): part = jnp.transpose(rows_h.reshape(rows_piece, ncols, cd_dev), (1, 0, 2))  29.3 us
    dot_general x2, matrix products, on_device(): jnp.dot(masked_t, masked_v, preferred_element_type=jnp.float32)  28 us
    all_to_all x2, starting transfers between devices, on_device(): panel = lax.all_to_all(part, 'col', split_axis=0, concat_axis=0, tiled=True)  11.9 us
    slice x2, local copies, waits for them, and re-layouts, on_device(): rows_h = source_rows[h * rows_piece:(h + 1) * rows_piece]  8.52 us
  transfers between devices with their start and end apart: 2, of which 2 were waited for; matrix products, arithmetic and copies ran while one was open for 14% of the time, Pallas kernels for 0%

profile of v12, /device:TPU:0, one launch (start us, length us, event | category | flops | bytes accessed | tf_op | source)
XLA Modules:
  0.0 256.1 jit_solution(17365990551104902757)
XLA Ops:
  0.0 4.2 %slice.6 = bf16[24,80000]{1,0:T(8,128)(2,1)} slice(bf16[48,80000]{1,0:T(8,128)(2,1)} %param.5), slice={[0:24], [0:80000]} | slice | bytes 7680000 | tf_op jit(solution)/shard_map/slice | solution.py:41
  4.2 8.4 %reshape.255 = bf16[24,16,5000]{2,1,0:T(8,128)(2,1)} reshape(bf16[24,80000]{1,0:T(8,128)(2,1)} %slice.6) | data formatting | bytes 7680000 | tf_op jit(solution)/shard_map/reshape | solution.py:42
  12.7 6.2 %copy.13 = bf16[24,16,5000]{2,0,1:T(8,128)(2,1)} copy(bf16[24,16,5000]{2,1,0:T(8,128)(2,1)} %reshape.255) | data formatting | bytes 7680000 | tf_op jit(solution)/shard_map/reshape | solution.py:42
  18.8 7.2 %all-to-all-start = ((bf16[16,24,5000]{2,1,0:T(8,128)(2,1)}), bf16[16,24,5000]{2,1,0:T(8,128)(2,1)}, u32[]{:S(2)}, u32[]{:S(2)}) async-start(bf16[16,24,5000]{2,1,0:T(8,128)(2,1)} %bitcast.11), calls=%async_computation | async-start | bytes 7864320 | tf_op jit(solution)/shard_map/all_to_all | solution.py:44
  26.0 0.1 sign_compare_fusion.2
  26.1 0.1 ne.241
  26.2 0.1 sign_compare_fusion.1
  26.3 0.1 ne.253
  26.4 0.1 fusion.32
  26.5 0.1 div.77
  26.6 0.1 rem.151
  26.7 0.1 fusion.34
  26.7 0.1 div.73
  26.8 0.1 rem.144
  26.9 4.3 %slice.7 = bf16[24,80000]{1,0:T(8,128)(2,1)} slice(bf16[48,80000]{1,0:T(8,128)(2,1)} %param.5), slice={[24:48], [0:80000]} | slice | bytes 7680000 | tf_op jit(solution)/shard_map/slice | solution.py:41
  31.2 8.4 %reshape.257 = bf16[24,16,5000]{2,1,0:T(8,128)(2,1)} reshape(bf16[24,80000]{1,0:T(8,128)(2,1)} %slice.7) | data formatting | bytes 7680000 | tf_op jit(solution)/shard_map/reshape | solution.py:42
  39.6 0.0 copy-start
  39.6 6.3 %copy.12 = bf16[24,16,5000]{2,0,1:T(8,128)(2,1)} copy(bf16[24,16,5000]{2,1,0:T(8,128)(2,1)} %reshape.257) | data formatting | bytes 7680000 | tf_op jit(solution)/shard_map/reshape | solution.py:42
  45.9 0.0 copy-done
  45.9 0.2 select_reduce_fusion
  46.2 0.2 compare_reduce_fusion
  46.3 0.2 fusion.24
  46.5 0.1 sign_compare_fusion.3
  46.6 0.1 fusion.37
  46.7 0.0 copy-start.2
  46.7 0.0 copy-start.1
  46.7 28.3 %all-to-all-done = bf16[16,24,5000]{2,1,0:T(8,128)(2,1)} async-done(((bf16[16,24,5000]{2,1,0:T(8,128)(2,1)}), bf16[16,24,5000]{2,1,0:T(8,128)(2,1)}, u32[]{:S(2)}, u32[]{:S(2)}) %all-to-all-start) | async-done | bytes 3840032 | tf_op jit(solution)/shard_map/all_to_all | solution.py:44
  75.0 4.7 %all-to-all-start.1 = ((bf16[16,24,5000]{2,1,0:T(8,128)(2,1)}), bf16[16,24,5000]{2,1,0:T(8,128)(2,1)}, u32[]{:S(2)}, u32[]{:S(2)}) async-start(bf16[16,24,5000]{2,1,0:T(8,128)(2,1)} %bitcast.10), calls=%async_computation.1 | async-start | bytes 7864320 | tf_op jit(solution)/shard_map/all_to_all | solution.py:44
  79.7 0.0 copy-done.2
  79.7 0.2 convert_reduce_fusion.9
  79.9 0.1 broadcast_in_dim.28
  80.0 0.1 reshape.254
  80.1 0.1 ne.238
  80.2 0.1 rem.138
  80.3 0.1 div.71
  80.3 0.1 convert_reduce_fusion.5
  80.5 0.0 copy-done.1
  80.5 0.2 convert_reduce_fusion.4
  80.7 0.1 convert_reduce_fusion.2
  80.8 0.2 convert_reduce_fusion
  81.1 13.3 %fusion.1 = f32[384,1600]{0,1:T(8,128)S(1)} fusion(bf16[5000,1600]{0,1:T(8,128)(2,1)} %param.6, s32[5000]{0:T(1024)S(1)} %xor.33, s32[1600]{0:T(1024)S(1)} %xor.34, bf16[384,5000]{1,0:T(8,128)(2,1)} %bitcast.1, s32[384]{0:T(512)S(1)} %xor.32), kind=kOutput, calls=%fused_computation.4 | convolution fusion | flops 6163840000 | bytes 22325536 | tf_op jit(solution)/shard_map/dot_general | solution.py:55
  94.4 34.1 %all-to-all-done.1 = bf16[16,24,5000]{2,1,0:T(8,128)(2,1)} async-done(((bf16[16,24,5000]{2,1,0:T(8,128)(2,1)}), bf16[16,24,5000]{2,1,0:T(8,128)(2,1)}, u32[]{:S(2)}, u32[]{:S(2)}) %all-to-all-start.1) | async-done | bytes 3840032 | tf_op jit(solution)/shard_map/all_to_all | solution.py:44
  128.5 14.6 %fusion = f32[384,1600]{0,1:T(8,128)} fusion(bf16[5000,1600]{0,1:T(8,128)(2,1)} %param.6, s32[5000]{0:T(1024)S(1)} %xor.33, s32[1600]{0:T(1024)S(1)} %xor.34, bf16[384,5000]{1,0:T(8,128)(2,1)} %bitcast.3, s32[384]{0:T(512)S(1)} %xor.35), kind=kOutput, calls=%fused_computation.3 | convolution fusion | flops 6163840000 | bytes 22325536 | tf_op jit(solution)/shard_map/dot_general | solution.py:55
  143.1 108.9 %all-reduce.2 = (bf16[384,1600]{0,1:T(8,128)(2,1)}, bf16[384,1600]{0,1:T(8,128)(2,1)}) all-reduce(f32[384,1600]{0,1:T(8,128)S(1)} %fusion.1, f32[384,1600]{0,1:T(8,128)} %fusion), channel_id=1, replica_groups=mesh['row'=8,'col'=16] {'row','col'}, use_global_device_ids=true, to_apply=%region_11.12 | all-reduce | flops 1228800 | bytes 7372800 | tf_op jit(solution)/shard_map/psum | solution.py:62
  252.0 1.7 fusion.12
  253.7 2.4 fusion.6
  (16 shorter events, 0.1 us)
Async XLA Ops:
  18.8 56.2 %all-to-all-start = ((bf16[16,24,5000]{2,1,0:T(8,128)(2,1)}), bf16[16,24,5000]{2,1,0:T(8,128)(2,1)}, u32[]{:S(2)}, u32[]{:S(2)}) async-start(bf16[16,24,5000]{2,1,0:T(8,128)(2,1)} %bitcast.11), calls=%async_computation | async-start | bytes 7864320 | tf_op jit(solution)/shard_map/all_to_all | solution.py:44
  39.6 6.3 %copy-start = (s32[384]{0:T(512)S(1)}, s32[384]{0:T(512)}, u32[]{:S(2)}) copy-start(s32[384]{0:T(512)} %param.9) | copy-start | bytes 4612
  46.7 33.0 %copy-start.2 = (s32[120]{0:T(128)S(1)}, s32[120]{0:T(128)}, u32[]{:S(2)}) copy-start(s32[120]{0:T(128)} %param.7) | copy-start | bytes 1444
  46.7 33.8 %copy-start.1 = (s32[800]{0:T(1024)S(1)}, s32[800]{0:T(1024)}, u32[]{:S(2)}) copy-start(s32[800]{0:T(1024)} %param.8) | copy-start | bytes 9604
  75.0 53.5 %all-to-all-start.1 = ((bf16[16,24,5000]{2,1,0:T(8,128)(2,1)}), bf16[16,24,5000]{2,1,0:T(8,128)(2,1)}, u32[]{:S(2)}, u32[]{:S(2)}) async-start(bf16[16,24,5000]{2,1,0:T(8,128)(2,1)} %bitcast.10), calls=%async_computation.1 | async-start | bytes 7864320 | tf_op jit(solution)/shard_map/all_to_all | solution.py:44
